TPU v7x, 256 devices: a whole 4x4x8 slice. The times are simulated.
256 devices in a mesh: dp: 8 (over z), seq: 32 (over y, x, core).
Axes of the slice: x: 4, y: 4, z: 8, core: 2. Of those that a mesh axis runs over, the one named last changes fastest.
Arguments:
- tokens: int32 [8, 16384], P('dp', 'seq'), may hold values from 0 to 3
- embed_table: bfloat16 [4, 768], replicated, may hold values from -6 to 6
- mix_weight: bfloat16 [2, 768, 768], replicated, may hold values from -0.21875 to 0.21875
- kernels: bfloat16 [2, 3, 768], replicated, may hold values from -3.5 to 3.5
- donor_proj: bfloat16 [768, 256], replicated, may hold values from -0.21875 to 0.21875
- acceptor_proj: bfloat16 [768, 256], replicated, may hold values from -0.21875 to 0.21875
- tissue_scale: float32 [4, 256], replicated, may hold values from -0.375 to 0.375
- junction_dest: int32 [8, 8192, 1], P('dp', 'seq'), may hold values from 0 to 31; in each aligned block of 256 rows (0 to 255, 256 to 511, ..., all dimensions but the last counted through in order) at most 16 rows name the same one
- donor_offset: int32 [8, 8192], P('dp', 'seq'), may hold values from 0 to 511
- acceptor_offset: int32 [8, 8192], P('dp', 'seq'), may hold values from 0 to 511
- tissue_ids: int32 [8, 8192], P('dp', 'seq'), may hold values from 0 to 3
- targets: float32 [8, 8192], P('dp', 'seq'), may hold values from -6 to 6
Outputs:
- features: bfloat16 [8, 16384, 768], P('dp', 'seq')
- input_grad: bfloat16 [8, 16384, 768], P('dp', 'seq')
- mix_grad: float32 [2, 768, 768], P(None, 'dp')
- kernel_grad: float32 [2, 3, 768], P(None, None, 'dp')
- embed_grad: float32 [4, 768], P(None, 'dp')
- donor_grad: float32 [768, 256], P('dp')
- acceptor_grad: float32 [768, 256], P('dp')
- tissue_grad: float32 [4, 256], P(None, 'dp')
Inputs may be any that keep to these rules, and one draw needn't show every extreme that they name: `junction_dest`: in each aligned block of 256 rows (the junctions of one device) no value appears more than 16 times, a bound that some block reaches.
All inputs are finite; a program needn't handle non-finite values.
Results may differ from a plain program's by a relative error of at most 0.02.
Values may be sent and summed in bfloat16 or wider, within the bound.
No kernel may reach another device: no remote copies, remote signals or barrier semaphores. Data moves between devices by JAX's collectives and lax.ppermute only.
A program may use at most 64 MiB of HBM per device.

v0:
```python
import jax
import jax.numpy as jnp
from jax import lax
from jax.sharding import PartitionSpec as P

FIRST_DILATION = 16
SECOND_DILATION = 128


epsilon = 1e-06


def padded(cells, sides, width):
    for axis, dim in sides:
        count = lax.axis_size(axis)
        ends = count - 1
        head = lax.slice_in_dim(cells, 0, width, axis=dim)
        tail = lax.slice_in_dim(cells, cells.shape[dim] - width, cells.shape[dim], axis=dim)
        cells = jnp.concatenate(
            [
                lax.ppermute(tail, axis, [(i, (i + 1) % count) for i in range(ends)]),
                cells,
                lax.ppermute(head, axis, [((i + 1) % count, i) for i in range(ends)]),
            ],
            axis=dim,
        )
    return cells


def normalize(stream_wide):
    inv_rms = lax.rsqrt(jnp.mean(stream_wide * stream_wide, axis=-1, keepdims=True) + epsilon)
    return (stream_wide * inv_rms, inv_rms)


def gelu_tanh(values):
    return jax.nn.gelu(values, approximate=True)


def norm_halo(norm_low, dilation):
    return padded(norm_low, (("seq", 0),), dilation)


def grad_halo(conv_low, dilation):
    return padded(conv_low, (("seq", 0),), dilation)


def per_device(
    tokens,
    embed_table,
    mix_weight,
    kernels,
    donor_proj,
    acceptor_proj,
    tissue_scale,
    junction_dest,
    donor_offset,
    acceptor_offset,
    tissue_ids,
    targets,
):
    length = tokens.shape[1]
    tok_row = tokens[0]
    vocab_hits = tok_row[:, None] == jnp.arange(embed_table.shape[0], dtype=jnp.int32)[None, :]
    stream = jnp.dot(
        vocab_hits.astype(jnp.bfloat16), embed_table, preferred_element_type=jnp.float32
    ).astype(jnp.bfloat16)
    dilation_sizes = (FIRST_DILATION, SECOND_DILATION)
    saved = []
    for layer_index in range(2):
        dilation = dilation_sizes[layer_index]
        stream_wide = stream.astype(jnp.float32)
        normed, inv_rms = normalize(stream_wide)
        norm_low = normed.astype(jnp.bfloat16)
        padded_input = norm_halo(norm_low, dilation)
        padded_wide = padded_input.astype(jnp.float32)
        kernel_wide = kernels[layer_index].astype(jnp.float32)
        conv_out = (
            kernel_wide[0] * padded_wide[:length]
            + kernel_wide[1] * padded_wide[dilation : dilation + length]
            + kernel_wide[2] * padded_wide[2 * dilation :]
        )
        activated = gelu_tanh(conv_out).astype(jnp.bfloat16)
        updated_params = stream_wide + jnp.dot(
            activated, mix_weight[layer_index], preferred_element_type=jnp.float32
        )
        saved.append((normed, inv_rms, padded_input, conv_out, activated))
        stream = updated_params.astype(jnp.bfloat16)
    dest = junction_dest[0, :, 0]
    donor_rows = donor_offset[0]
    accept_rows = acceptor_offset[0]
    tissue_row = tissue_ids[0]
    count = lax.axis_size("seq")
    capacity = 2 * dest.shape[0] // count
    dest_hits = (dest[:, None] == jnp.arange(count, dtype=jnp.int32)[None, :]).astype(jnp.int32)
    before = jnp.cumsum(dest_hits, axis=0) - dest_hits
    slot = jnp.sum(before * dest_hits, axis=1)
    request = jnp.full((count, capacity), -1, jnp.int32).at[dest, slot].set(accept_rows)
    asked = lax.all_to_all(request, "seq", split_axis=0, concat_axis=0, tiled=True)
    valid = (asked >= 0).reshape(-1)
    asked_rows = jnp.where(valid, asked.reshape(-1), 0)
    accepted = stream[asked_rows]
    accept_emb = jnp.dot(accepted, acceptor_proj, preferred_element_type=jnp.float32)
    answer = (
        jnp.where(valid[:, None], accept_emb, 0.0).astype(jnp.bfloat16).reshape(count, capacity, -1)
    )
    returned = lax.all_to_all(answer, "seq", split_axis=0, concat_axis=0, tiled=True)
    accept_wide = returned[dest, slot].astype(jnp.float32)
    donors = stream[donor_rows]
    donor_emb = jnp.dot(donors, donor_proj, preferred_element_type=jnp.float32)
    tissue_hits = (
        tissue_row[:, None] == jnp.arange(tissue_scale.shape[0], dtype=jnp.int32)[None, :]
    ).astype(jnp.float32)
    tissue_rows = jnp.dot(tissue_hits, tissue_scale, precision=lax.Precision.HIGHEST)
    score = jnp.sum(donor_emb * accept_wide * tissue_rows, axis=-1)
    misfit = score - targets[0]
    donor_back = (misfit[:, None] * accept_wide * tissue_rows).astype(jnp.bfloat16)
    accept_back = (misfit[:, None] * donor_emb * tissue_rows).astype(jnp.bfloat16)
    tissue_part = jnp.dot(
        tissue_hits.T, misfit[:, None] * donor_emb * accept_wide, precision=lax.Precision.HIGHEST
    )
    donor_part = jnp.dot(donors.T, donor_back, preferred_element_type=jnp.float32)
    back_buffer = (
        jnp.zeros((count, capacity, accept_back.shape[1]), jnp.bfloat16)
        .at[dest, slot]
        .set(accept_back)
    )
    accept_grads = lax.all_to_all(
        back_buffer, "seq", split_axis=0, concat_axis=0, tiled=True
    ).reshape(count * capacity, -1)
    accept_part = jnp.dot(accepted.T, accept_grads, preferred_element_type=jnp.float32)
    upstream = jnp.zeros((length, stream.shape[1]), jnp.float32)
    upstream = upstream.at[donor_rows].add(
        jnp.dot(donor_back, donor_proj.T, preferred_element_type=jnp.float32)
    )
    upstream = upstream.at[asked_rows].add(
        jnp.dot(accept_grads, acceptor_proj.T, preferred_element_type=jnp.float32)
    )
    mix_parts = [None, None]
    kernel_parts = [None, None]
    for layer_index in (1, 0):
        dilation = dilation_sizes[layer_index]
        normed, inv_rms, stored, conv_out, activated = saved[layer_index]
        upstream_low = upstream.astype(jnp.bfloat16)
        mix_parts[layer_index] = jnp.dot(
            activated.T, upstream_low, preferred_element_type=jnp.float32
        )
        act_grad = jnp.dot(
            upstream_low, mix_weight[layer_index].T, preferred_element_type=jnp.float32
        )
        gelu_value, pullback = jax.vjp(gelu_tanh, conv_out)
        conv_low = pullback(act_grad)[0].astype(jnp.bfloat16)
        padded_wide = stored.astype(jnp.float32)
        grad_padded = grad_halo(conv_low, dilation).astype(jnp.float32)
        conv_wide = grad_padded[dilation : dilation + length]
        kernel_parts[layer_index] = jnp.stack(
            [
                jnp.sum(conv_wide * padded_wide[:length], axis=0),
                jnp.sum(conv_wide * padded_wide[dilation : dilation + length], axis=0),
                jnp.sum(conv_wide * padded_wide[2 * dilation :], axis=0),
            ]
        )
        kernel_wide = kernels[layer_index].astype(jnp.float32)
        norm_grad = (
            kernel_wide[0] * grad_padded[2 * dilation :]
            + kernel_wide[1] * conv_wide
            + kernel_wide[2] * grad_padded[:length]
        )
        upstream = upstream + inv_rms * (
            norm_grad - normed * jnp.mean(norm_grad * normed, axis=-1, keepdims=True)
        )
    embed_part = jnp.dot(
        vocab_hits.astype(jnp.float32).T, upstream, precision=lax.Precision.HIGHEST
    )
    mix_local = jnp.stack(mix_parts)
    kernel_local = jnp.stack(kernel_parts)
    summed_output = lax.psum(
        (mix_local, donor_part, accept_part, kernel_local, embed_part, tissue_part), "seq"
    )
    mix_grad, donor_grad, accept_grad, kernel_grad, embed_grad, tissue_grad = (
        lax.psum_scatter(summed_output[0], "dp", scatter_dimension=1, tiled=True),
        lax.psum_scatter(summed_output[1], "dp", scatter_dimension=0, tiled=True),
        lax.psum_scatter(summed_output[2], "dp", scatter_dimension=0, tiled=True),
        lax.psum_scatter(summed_output[3], "dp", scatter_dimension=2, tiled=True),
        lax.psum_scatter(summed_output[4], "dp", scatter_dimension=1, tiled=True),
        lax.psum_scatter(summed_output[5], "dp", scatter_dimension=1, tiled=True),
    )
    features = stream[None]
    input_grad = upstream.astype(jnp.bfloat16)[None]
    return (
        features,
        input_grad,
        mix_grad,
        kernel_grad,
        embed_grad,
        donor_grad,
        accept_grad,
        tissue_grad,
    )


def solution(mesh):
    placed = (
        P("dp", "seq"),
        P(),
        P(),
        P(),
        P(),
        P(),
        P(),
        P("dp", "seq", None),
        P("dp", "seq"),
        P("dp", "seq"),
        P("dp", "seq"),
        P("dp", "seq"),
    )
    return jax.shard_map(
        per_device,
        mesh=mesh,
        in_specs=placed,
        out_specs=(
            P("dp", "seq", None),
            P("dp", "seq", None),
            P(None, "dp", None),
            P(None, None, "dp"),
            P(None, "dp"),
            P("dp", None),
            P("dp", None),
            P(None, "dp"),
        ),
        check_vma=False,
    )
```

profile of v0, /device:TPU:1, one launch (start us, length us, event | category | flops | bytes accessed | tf_op | source)
XLA Modules:
  0.0 501.1 jit_solution(18206342228674541994)
XLA Ops:
  10.2 21.7 %scatter_fusion = s32[32,16]{0,1:T(8,128)S(1)} fusion(s32[32,16]{0,1:T(8,128)S(1)} %broadcast_in_dim.26, s32[256]{0:T(256)S(1)} %bitcast.95, s32[256]{0:T(256)} %bitcast.115), kind=kCustom, calls=%fused_computation.3 | custom fusion | bytes 5120 | tf_op jit(solution)/shard_map/scatter | solution.py:97
  32.6 8.6 %all-to-all-start = ((s32[32,1,16]{2,1,0:T(1,128)}), s32[32,1,16]{2,1,0:T(1,128)S(1)}, u32[]{:S(2)}, u32[]{:S(2)}) async-start(s32[32,1,16]{2,1,0:T(1,128)} %copy.28), calls=%async_computation | async-start | bytes 32768 | tf_op jit(solution)/shard_map/all_to_all | solution.py:98
  42.0 3.5 collective-permute-start
  45.5 1.9 collective-permute-start.1
  55.2 2.5 collective-permute-start.2
  60.2 4.4 collective-permute-done.3
  68.7 2.0 gather_fusion.1
  71.8 10.6 %all-to-all-start.1 = ((bf16[32,16,256]{2,1,0:T(8,128)(2,1)}), bf16[32,16,256]{2,1,0:T(8,128)(2,1)S(1)}, u32[]{:S(2)}, u32[]{:S(2)}) async-start(bf16[32,16,256]{2,1,0:T(8,128)(2,1)} %bitcast.15), calls=%async_computation.1 | async-start | bytes 524288 | tf_op jit(solution)/shard_map/all_to_all | solution.py:106
  84.1 7.2 %all-to-all-done.1 = bf16[32,16,256]{2,1,0:T(8,128)(2,1)S(1)} async-done(((bf16[32,16,256]{2,1,0:T(8,128)(2,1)}), bf16[32,16,256]{2,1,0:T(8,128)(2,1)S(1)}, u32[]{:S(2)}, u32[]{:S(2)}) %all-to-all-start.1) | async-done | bytes 262176 | tf_op jit(solution)/shard_map/all_to_all | solution.py:106
  95.7 29.5 %scatter_fusion.1 = bf16[32,16,256]{2,1,0:T(8,128)(2,1)} fusion(bf16[32,16,256]{2,1,0:T(8,128)(2,1)} %broadcast_in_dim.29, s32[256]{0:T(256)S(1)} %bitcast.96, bf16[256,256]{1,0:T(8,128)(2,1)S(1)} %copy.30), kind=kCustom, calls=%fused_computation.5 | custom fusion | bytes 395264 | tf_op jit(solution)/shard_map/scatter | solution.py:125
  125.1 3.8 all-to-all-start.2
  130.4 3.2 scatter_custom_fusion.1
  133.5 4.3 all-to-all-done.2
  139.4 5.3 %scatter_fusion.2 = f32[512,768]{1,0:T(8,128)S(1)} fusion(f32[512,768]{1,0:T(8,128)S(1)} %scatter_custom_fusion.1, s32[512]{0:T(512)S(1)} %bitcast.104, f32[512,768]{1,0:T(8,128)} %fusion.85), kind=kCustom, calls=%fused_computation.6 | custom fusion | flops 393216 | bytes 4720640 | tf_op jit(solution)/shard_map/scatter-add | solution.py:135
  144.8 3.3 fusion.27
  149.7 2.2 collective-permute-start.4
  152.0 2.7 collective-permute-start.5
  156.1 2.5 convolution_bitcast_fusion
  164.9 2.5 pad_maximum_fusion
  168.8 2.8 fusion.20
  171.6 2.9 collective-permute-start.6
  174.5 2.1 collective-permute-start.7
  183.8 2.5 convolution_bitcast_fusion.2
  187.0 2.0 copy.32
  189.0 2.3 reshape.248
  191.4 65.2 %reduce-scatter.13.cloned.1.call-done = f32[2,96,768]{2,1,0:T(8,128)} async-done(((f32[2,768,768]{2,1,0:T(8,128)}), f32[2,96,768]{2,1,0:T(8,128)}) %reduce-scatter.13.cloned.1.call-update) | async-done | bytes 589840 | tf_op jit(solution)/shard_map/reduce_scatter | solution.py:180
  256.7 32.5 %reduce-scatter.23.cloned.1.call-done = f32[32,4]{1,0:T(8,128)} async-done(((f32[256,4]{1,0:T(8,128)}), f32[32,4]{1,0:T(8,128)}) %reduce-scatter.23.cloned.1.call-update) | async-done | bytes 528
  290.0 2.4 convert_bitcast_fusion
  292.4 35.8 %reduce-scatter.21.cloned.1.call-done = f32[96,4]{1,0:T(8,128)} async-done(((f32[768,4]{1,0:T(8,128)}), f32[96,4]{1,0:T(8,128)}) %reduce-scatter.21.cloned.1.call-update) | async-done | bytes 1552
  329.1 38.2 %reduce-scatter.19.cloned.1.call-done = f32[96,6]{1,0:T(8,128)} async-done(((f32[768,6]{1,0:T(8,128)}), f32[96,6]{1,0:T(8,128)}) %reduce-scatter.19.cloned.1.call-update) | async-done | bytes 2320
  368.3 69.4 %all-reduce = (f32[2,3,96]{2,1,0:T(4,128)S(1)}, f32[4,96]{1,0:T(4,128)}, f32[4,32]{1,0:T(4,128)}) all-reduce(f32[2,3,96]{2,1,0:T(4,128)S(1)} %copy.33, f32[4,96]{1,0:T(4,128)S(1)} %copy.35, f32[4,32]{1,0:T(4,128)S(1)} %copy.37), channel_id=1, replica_groups=mesh['dp'=8,'seq'=32] {'seq'}, use_global_device_ids=true, to_apply=%region_20.21 | all-reduce | flops 1088 | bytes 8704 | tf_op jit(solution)/shard_map/psum | solution.py:176
  438.3 51.0 %all-reduce.4.cloned.1.call-done = (f32[2,96,768]{2,1,0:T(8,128)}, f32[96,256]{1,0:T(8,128)}, f32[96,256]{1,0:T(8,128)}) async-done(((f32[2,96,768]{2,1,0:T(8,128)}, f32[96,256]{1,0:T(8,128)}, f32[96,256]{1,0:T(8,128)}), (f32[2,96,768]{2,1,0:T(8,128)}, f32[96,256]{1,0:T(8,128)}, f32[96,256]{1,0:T(8,128)})) %all-reduce.4.cloned.1.call-update) | async-done | bytes 786448 | tf_op jit(solution)/shard_map/psum | solution.py:176
  (204 shorter events, 55.2 us)
Async XLA Ops:
  7.2 63.6 %copy-start = (bf16[768,256]{1,0:T(8,128)(2,1)S(1)}, bf16[768,256]{1,0:T(8,128)(2,1)}, u32[]{:S(2)}) copy-start(bf16[768,256]{1,0:T(8,128)(2,1)} %param.17) | copy-start | bytes 1179652
  7.2 34.0 %copy-start.51 = (bf16[4,768]{1,0:T(4,128)(2,1)S(1)}, bf16[4,768]{1,0:T(4,128)(2,1)}, u32[]{:S(2)}) copy-start(bf16[4,768]{1,0:T(4,128)(2,1)} %param.13) | copy-start | bytes 18436
  7.2 34.0 %copy-start.45 = (s32[1,512]{1,0:T(1,128)S(1)}, s32[1,512]{1,0:T(1,128)}, u32[]{:S(2)}) copy-start(s32[1,512]{1,0:T(1,128)} %param.12) | copy-start | bytes 6148
  31.9 15.5 %copy-start.48 = (s32[1,256]{1,0:T(1,128)S(1)}, s32[1,256]{1,0:T(1,128)}, u32[]{:S(2)}) copy-start(s32[1,256]{1,0:T(1,128)} %param.20) | copy-start | bytes 3076
  31.9 16.1 %copy-start.28 = (bf16[2,3,768]{2,0,1:T(2,128)(2,1)S(1)}, bf16[2,3,768]{2,0,1:T(2,128)(2,1)}, u32[]{:S(2)}) copy-start(bf16[2,3,768]{2,0,1:T(2,128)(2,1)} %param.15) | copy-start | bytes 27652
  32.6 15.5 %all-to-all-start = ((s32[32,1,16]{2,1,0:T(1,128)}), s32[32,1,16]{2,1,0:T(1,128)S(1)}, u32[]{:S(2)}, u32[]{:S(2)}) async-start(s32[32,1,16]{2,1,0:T(1,128)} %copy.28), calls=%async_computation | async-start | bytes 32768 | tf_op jit(solution)/shard_map/all_to_all | solution.py:98
  42.0 7.5 %collective-permute-start = (bf16[16,768]{1,0:T(8,128)(2,1)S(1)}, bf16[16,768]{1,0:T(8,128)(2,1)S(1)}, u32[]{:S(2)}, u32[]{:S(2)}) collective-permute-start(bf16[16,768]{1,0:T(8,128)(2,1)S(1)} %get-tuple-element.58), channel_id=1, source_target_pairs={{0,1},{1,2},{2,3},{3,4},{4,5},{5,6},{6,7},{7,8},{8,9},{9,10},{10,1... | collective-permute-start | bytes 73736 | tf_op jit(solution)/shard_map/ppermute | solution.py:21
  45.5 5.1 %collective-permute-start.1 = (bf16[16,768]{1,0:T(8,128)(2,1)S(1)}, bf16[16,768]{1,0:T(8,128)(2,1)S(1)}, u32[]{:S(2)}, u32[]{:S(2)}) collective-permute-start(bf16[16,768]{1,0:T(8,128)(2,1)S(1)} %get-tuple-element.59), channel_id=1, source_target_pairs={{1,0},{2,1},{3,2},{4,3},{5,4},{6,5},{7,6},{8,7},{9,8},{10,9},{11,1... | collective-permute-start | bytes 73736 | tf_op jit(solution)/shard_map/ppermute | solution.py:23
  48.1 16.8 %copy-start.29 = (f32[768]{0:T(1024)}, f32[768]{0:T(1024)S(1)}, u32[]{:S(2)}) copy-start(f32[768]{0:T(1024)S(1)} %get-tuple-element.30) | copy-start | bytes 9220
  48.1 16.8 %copy-start.31 = (f32[768]{0:T(1024)}, f32[768]{0:T(1024)S(1)}, u32[]{:S(2)}) copy-start(f32[768]{0:T(1024)S(1)} %get-tuple-element.31) | copy-start | bytes 9220
  48.1 16.8 %copy-start.33 = (f32[768]{0:T(1024)}, f32[768]{0:T(1024)S(1)}, u32[]{:S(2)}) copy-start(f32[768]{0:T(1024)S(1)} %get-tuple-element.32) | copy-start | bytes 9220
  54.3 106.2 %copy-start.13 = (bf16[512,768]{1,0:T(8,128)(2,1)}, bf16[512,768]{1,0:T(8,128)(2,1)S(1)}, u32[]{:S(2)}) copy-start(bf16[512,768]{1,0:T(8,128)(2,1)S(1)} %get-tuple-element.67) | copy-start | bytes 2359300
  55.2 5.1 %collective-permute-start.2 = (bf16[128,768]{1,0:T(8,128)(2,1)S(1)}, bf16[128,768]{1,0:T(8,128)(2,1)S(1)}, u32[]{:S(2)}, u32[]{:S(2)}) collective-permute-start(bf16[128,768]{1,0:T(8,128)(2,1)S(1)} %get-tuple-element.56), channel_id=1, source_target_pairs={{0,1},{1,2},{2,3},{3,4},{4,5},{5,6},{6,7},{7,8},{8,9},{9,10},{10,1... | collective-permute-start | bytes 589832 | tf_op jit(solution)/shard_map/ppermute | solution.py:21
  57.7 7.0 %collective-permute-start.3 = (bf16[128,768]{1,0:T(8,128)(2,1)S(1)}, bf16[128,768]{1,0:T(8,128)(2,1)S(1)}, u32[]{:S(2)}, u32[]{:S(2)}) collective-permute-start(bf16[128,768]{1,0:T(8,128)(2,1)S(1)} %get-tuple-element.57), channel_id=1, source_target_pairs={{1,0},{2,1},{3,2},{4,3},{5,4},{6,5},{7,6},{8,7},{9,8},{10,9},{11,1... | collective-permute-start | bytes 589832 | tf_op jit(solution)/shard_map/ppermute | solution.py:23
  68.7 13.8 %copy-start.1 = (bf16[512,768]{1,0:T(8,128)(2,1)}, bf16[512,768]{1,0:T(8,128)(2,1)S(1)}, u32[]{:S(2)}) copy-start(bf16[512,768]{1,0:T(8,128)(2,1)S(1)} %fusion.31) | copy-start | bytes 2359300
  70.7 11.8 %copy-start.16 = (bf16[512,768]{1,0:T(8,128)(2,1)}, bf16[512,768]{1,0:T(8,128)(2,1)S(1)}, u32[]{:S(2)}) copy-start(bf16[512,768]{1,0:T(8,128)(2,1)S(1)} %gather_fusion.1) | copy-start | bytes 2359300
  70.7 11.8 %copy-start.44 = (s32[256,1]{0,1:T(1,128)S(1)}, s32[256,1]{0,1:T(1,128)}, u32[]{:S(2)}) copy-start(s32[256,1]{0,1:T(1,128)} %compare_select_fusion.4) | copy-start | bytes 3076
  71.8 19.5 %all-to-all-start.1 = ((bf16[32,16,256]{2,1,0:T(8,128)(2,1)}), bf16[32,16,256]{2,1,0:T(8,128)(2,1)S(1)}, u32[]{:S(2)}, u32[]{:S(2)}) async-start(bf16[32,16,256]{2,1,0:T(8,128)(2,1)} %bitcast.15), calls=%async_computation.1 | async-start | bytes 524288 | tf_op jit(solution)/shard_map/all_to_all | solution.py:106
  82.4 108.9 %reduce-scatter.15.cloned.1.call-start = ((), (), s32[]{:S(2)}) async-start(), calls=%async_computation.10 | async-start | bytes 884736 | tf_op jit(solution)/shard_map/reduce_scatter | solution.py:181
  125.1 12.7 %all-to-all-start.2 = ((bf16[32,16,256]{2,1,0:T(8,128)(2,1)}), bf16[32,16,256]{2,1,0:T(8,128)(2,1)S(1)}, u32[]{:S(2)}, u32[]{:S(2)}) async-start(bf16[32,16,256]{2,1,0:T(8,128)(2,1)} %scatter_fusion.1), calls=%async_computation.2 | async-start | bytes 524288 | tf_op jit(solution)/shard_map/all_to_all | solution.py:127
  128.9 62.5 %reduce-scatter.17.cloned.1.call-start = ((), (), s32[]{:S(2)}) async-start(), calls=%async_computation.11 | async-start | bytes 884736 | tf_op jit(solution)/shard_map/reduce_scatter | solution.py:182
  149.7 8.9 %collective-permute-start.4 = (bf16[128,768]{1,0:T(8,128)(2,1)}, bf16[128,768]{1,0:T(8,128)(2,1)}, u32[]{:S(2)}, u32[]{:S(2)}) collective-permute-start(bf16[128,768]{1,0:T(8,128)(2,1)} %get-tuple-element.54), channel_id=1, source_target_pairs={{0,1},{1,2},{2,3},{3,4},{4,5},{5,6},{6,7},{7,8},{8,9},{9,10},{10,1... | collective-permute-start | bytes 589832 | tf_op jit(solution)/shard_map/ppermute | solution.py:21
  152.0 7.3 %collective-permute-start.5 = (bf16[128,768]{1,0:T(8,128)(2,1)}, bf16[128,768]{1,0:T(8,128)(2,1)}, u32[]{:S(2)}, u32[]{:S(2)}) collective-permute-start(bf16[128,768]{1,0:T(8,128)(2,1)} %get-tuple-element.55), channel_id=1, source_target_pairs={{1,0},{2,1},{3,2},{4,3},{5,4},{6,5},{7,6},{8,7},{9,8},{10,9},{11,1... | collective-permute-start | bytes 589832 | tf_op jit(solution)/shard_map/ppermute | solution.py:23
  156.1 100.6 %reduce-scatter.13.cloned.1.call-start = ((), (), s32[]{:S(2)}) async-start(), calls=%async_computation.9 | async-start | bytes 5308416 | tf_op jit(solution)/shard_map/reduce_scatter | solution.py:180
  167.4 121.8 %reduce-scatter.23.cloned.1.call-start = ((), (), s32[]{:S(2)}) async-start(), calls=%async_computation.14 | async-start | bytes 147456
  171.6 8.2 %collective-permute-start.6 = (bf16[16,768]{1,0:T(8,128)(2,1)S(1)}, bf16[16,768]{1,0:T(8,128)(2,1)S(1)}, u32[]{:S(2)}, u32[]{:S(2)}) collective-permute-start(bf16[16,768]{1,0:T(8,128)(2,1)S(1)} %get-tuple-element.52), channel_id=1, source_target_pairs={{0,1},{1,2},{2,3},{3,4},{4,5},{5,6},{6,7},{7,8},{8,9},{9,10},{10,1... | collective-permute-start | bytes 73736 | tf_op jit(solution)/shard_map/ppermute | solution.py:21
  174.5 5.7 %collective-permute-start.7 = (bf16[16,768]{1,0:T(8,128)(2,1)S(1)}, bf16[16,768]{1,0:T(8,128)(2,1)S(1)}, u32[]{:S(2)}, u32[]{:S(2)}) collective-permute-start(bf16[16,768]{1,0:T(8,128)(2,1)S(1)} %get-tuple-element.53), channel_id=1, source_target_pairs={{1,0},{2,1},{3,2},{4,3},{5,4},{6,5},{7,6},{8,7},{9,8},{10,9},{11,1... | collective-permute-start | bytes 73736 | tf_op jit(solution)/shard_map/ppermute | solution.py:23
  177.7 150.5 %reduce-scatter.21.cloned.1.call-start = ((), (), s32[]{:S(2)}) async-start(), calls=%async_computation.13 | async-start | bytes 442368
  186.3 181.0 %reduce-scatter.19.cloned.1.call-start = ((), (), s32[]{:S(2)}) async-start(), calls=%async_computation.12 | async-start | bytes 442368
  187.0 103.0 %copy-start.7 = (f32[512,768]{1,0:T(8,128)S(1)}, f32[512,768]{1,0:T(8,128)}, u32[]{:S(2)}) copy-start(f32[512,768]{1,0:T(8,128)} %copy-done.6) | copy-start | bytes 4718596
  187.0 103.0 %copy-start.10 = (f32[512,768]{1,0:T(8,128)S(1)}, f32[512,768]{1,0:T(8,128)}, u32[]{:S(2)}) copy-start(f32[512,768]{1,0:T(8,128)} %copy-done.8) | copy-start | bytes 4718596
  191.3 298.0 %all-reduce.4.cloned.1.call-start = ((), (), s32[]{:S(2)}) async-start(), calls=%async_computation.15 | async-start | bytes 1572864 | tf_op jit(solution)/shard_map/psum | solution.py:176
  (38 other events, 166.1 us)
Sparse Core Ops, SparseCore 0:
  94.9 32.4 reduce-scatter.14
  156.2 34.0 reduce-scatter.16
  192.9 63.7 reduce-scatter.12
  259.0 30.1 reduce-scatter.22
  291.5 36.6 reduce-scatter.20
  331.1 36.1 reduce-scatter.18
  370.8 118.4 all-reduce.3
where the time goes:
time: 503 us; the launch traced here: 501 us
  waiting for transfers between devices  242 us (48%)
  local copies, waits for them, and re-layouts  82.7 us (16%)
  blocking collectives  69.4 us (14%)
  starting transfers between devices  43.1 us (9%)
  other arithmetic  26.2 us (5%)
  matrix products  23 us (5%)
  between operations  15.2 us (3%)
    unnamed x10, waiting for transfers between devices  107 us
    psum x1, blocking collectives, per_device(): lax.psum((mix_local, donor_part, accept_part, kernel_local, embed_part, t...  69.4 us
    reduce_scatter x1, waiting for transfers between devices, per_device(): lax.psum_scatter(summed_output[0], 'dp', scatter_dimension=1, tiled=True)  65.2 us
    psum x1, waiting for transfers between devices, per_device(): lax.psum((mix_local, donor_part, accept_part, kernel_local, embed_part, t...  51 us
    scatter x1, local copies, waits for them, and re-layouts, per_device(): back_buffer = jnp.zeros((count, capacity, accept_back.shape[1]), jnp.bflo...  29.5 us
    scatter x1, local copies, waits for them, and re-layouts, per_device(): jnp.full((count, capacity), -1, jnp.int32).at[dest, slot].set(accept_rows)  21.7 us
    unnamed x114, local copies, waits for them, and re-layouts  21.2 us
    ppermute x4, starting transfers between devices, padded(): lax.ppermute(tail, axis, [(i, (i + 1) % count) for i in range(ends)])  11.1 us
  transfers between devices with their start and end apart: 18, of which 12 were waited for; matrix products, arithmetic and copies ran while one was open for 17% of the time, Pallas kernels for 0%

commit v1 on v0

--- a/solution.py
+++ b/solution.py
@@ -94,7 +94,11 @@
     dest_hits = (dest[:, None] == jnp.arange(count, dtype=jnp.int32)[None, :]).astype(jnp.int32)
     before = jnp.cumsum(dest_hits, axis=0) - dest_hits
     slot = jnp.sum(before * dest_hits, axis=1)
-    request = jnp.full((count, capacity), -1, jnp.int32).at[dest, slot].set(accept_rows)
+    key = dest * capacity + slot
+    key_hits = key[:, None] == jnp.arange(count * capacity, dtype=jnp.int32)[None, :]
+    request = (
+        jnp.sum(jnp.where(key_hits, accept_rows[:, None] + 1, 0), axis=0) - 1
+    ).reshape(count, capacity)
     asked = lax.all_to_all(request, "seq", split_axis=0, concat_axis=0, tiled=True)
     valid = (asked >= 0).reshape(-1)
     asked_rows = jnp.where(valid, asked.reshape(-1), 0)
@@ -104,7 +108,10 @@
         jnp.where(valid[:, None], accept_emb, 0.0).astype(jnp.bfloat16).reshape(count, capacity, -1)
     )
     returned = lax.all_to_all(answer, "seq", split_axis=0, concat_axis=0, tiled=True)
-    accept_wide = returned[dest, slot].astype(jnp.float32)
+    key_low = key_hits.astype(jnp.bfloat16)
+    accept_wide = jnp.dot(
+        key_low, returned.reshape(count * capacity, -1), preferred_element_type=jnp.float32
+    )
     donors = stream[donor_rows]
     donor_emb = jnp.dot(donors, donor_proj, preferred_element_type=jnp.float32)
     tissue_hits = (
@@ -120,20 +127,25 @@
     )
     donor_part = jnp.dot(donors.T, donor_back, preferred_element_type=jnp.float32)
     back_buffer = (
-        jnp.zeros((count, capacity, accept_back.shape[1]), jnp.bfloat16)
-        .at[dest, slot]
-        .set(accept_back)
+        jnp.dot(key_low.T, accept_back, preferred_element_type=jnp.float32)
+        .astype(jnp.bfloat16)
+        .reshape(count, capacity, -1)
     )
     accept_grads = lax.all_to_all(
         back_buffer, "seq", split_axis=0, concat_axis=0, tiled=True
     ).reshape(count * capacity, -1)
     accept_part = jnp.dot(accepted.T, accept_grads, preferred_element_type=jnp.float32)
-    upstream = jnp.zeros((length, stream.shape[1]), jnp.float32)
-    upstream = upstream.at[donor_rows].add(
-        jnp.dot(donor_back, donor_proj.T, preferred_element_type=jnp.float32)
-    )
-    upstream = upstream.at[asked_rows].add(
-        jnp.dot(accept_grads, acceptor_proj.T, preferred_element_type=jnp.float32)
+    positions = jnp.arange(length, dtype=jnp.int32)[None, :]
+    donor_hits = (donor_rows[:, None] == positions).astype(jnp.float32)
+    asked_hits = ((asked_rows[:, None] == positions) & valid[:, None]).astype(jnp.float32)
+    upstream = jnp.dot(
+        donor_hits.T,
+        jnp.dot(donor_back, donor_proj.T, preferred_element_type=jnp.float32),
+        precision=lax.Precision.HIGHEST,
+    ) + jnp.dot(
+        asked_hits.T,
+        jnp.dot(accept_grads, acceptor_proj.T, preferred_element_type=jnp.float32),
+        precision=lax.Precision.HIGHEST,
     )
     mix_parts = [None, None]
     kernel_parts = [None, None]
@@ -171,18 +183,63 @@
     embed_part = jnp.dot(
         vocab_hits.astype(jnp.float32).T, upstream, precision=lax.Precision.HIGHEST
     )
-    mix_local = jnp.stack(mix_parts)
-    kernel_local = jnp.stack(kernel_parts)
-    summed_output = lax.psum(
-        (mix_local, donor_part, accept_part, kernel_local, embed_part, tissue_part), "seq"
-    )
-    mix_grad, donor_grad, accept_grad, kernel_grad, embed_grad, tissue_grad = (
-        lax.psum_scatter(summed_output[0], "dp", scatter_dimension=1, tiled=True),
-        lax.psum_scatter(summed_output[1], "dp", scatter_dimension=0, tiled=True),
-        lax.psum_scatter(summed_output[2], "dp", scatter_dimension=0, tiled=True),
-        lax.psum_scatter(summed_output[3], "dp", scatter_dimension=2, tiled=True),
-        lax.psum_scatter(summed_output[4], "dp", scatter_dimension=1, tiled=True),
-        lax.psum_scatter(summed_output[5], "dp", scatter_dimension=1, tiled=True),
+    groups = lax.axis_size("dp")
+    channels = stream.shape[1]
+    tissues, width = tissue_part.shape
+    rows = channels // groups
+    lanes = 128
+    tissue_cells = (
+        tissue_part.reshape(tissues, groups, width // groups)
+        .transpose(1, 0, 2)
+        .reshape(groups, -1)
+    )
+    tissue_cols = -(-tissue_cells.shape[1] // rows)
+    tissue_cells = jnp.pad(
+        tissue_cells, ((0, 0), (0, tissue_cols * rows - tissue_cells.shape[1]))
+    ).reshape(channels, tissue_cols)
+    kernel_local = jnp.stack(kernel_parts).reshape(-1, channels).T
+    small = jnp.concatenate([kernel_local, embed_part.T, tissue_cells], axis=1)
+    small_widths = [kernel_local.shape[1], embed_part.shape[0], tissue_cols]
+    big = [mix_parts[0], mix_parts[1], donor_part, accept_part]
+    big_total = sum(piece.shape[1] for piece in big)
+    total = -(-(big_total + small.shape[1]) // (2 * lanes)) * (2 * lanes)
+    packed = jnp.concatenate(
+        [piece.astype(jnp.bfloat16) for piece in big]
+        + [
+            jnp.pad(small, ((0, 0), (0, total - big_total - small.shape[1]))).astype(
+                jnp.bfloat16
+            )
+        ],
+        axis=1,
+    )
+    half = total // 2
+    core = lax.axis_index("seq") % 2
+    own = lax.dynamic_slice_in_dim(packed, core * half, half, axis=1)
+    other = lax.dynamic_slice_in_dim(packed, (1 - core) * half, half, axis=1)
+    partner = lax.ppermute(other, "seq", [(i, i ^ 1) for i in range(count)])
+    pair_sum = (own.astype(jnp.float32) + partner.astype(jnp.float32)).astype(jnp.bfloat16)
+    scattered = lax.psum_scatter(pair_sum, "dp", scatter_dimension=0, tiled=True)
+    share = rows // count
+    blocks = scattered.reshape(count, share * half)
+    exchanged = lax.all_to_all(blocks, "seq", split_axis=0, concat_axis=0, tiled=True)
+    by_core = exchanged.astype(jnp.float32).reshape(count // 2, 2, share * half)
+    own_sum = jnp.sum(by_core, axis=0).astype(jnp.bfloat16)
+    gathered = lax.all_gather(own_sum, "seq", axis=0, tiled=False)
+    summed = jnp.concatenate(
+        [gathered[:, 0].reshape(rows, half), gathered[:, 1].reshape(rows, half)], axis=1
+    ).astype(jnp.float32)
+    mix_grad = summed[:, : 2 * channels].reshape(rows, 2, channels).transpose(1, 0, 2)
+    proj_width = donor_part.shape[1]
+    donor_grad = summed[:, 2 * channels : 2 * channels + proj_width]
+    accept_grad = summed[:, 2 * channels + proj_width : big_total]
+    k0 = big_total
+    k1 = k0 + small_widths[0]
+    k2 = k1 + small_widths[1]
+    k3 = k2 + small_widths[2]
+    kernel_grad = summed[:, k0:k1].T.reshape(2, 3, rows)
+    embed_grad = summed[:, k1:k2].T
+    tissue_grad = (
+        summed[:, k2:k3].reshape(-1)[: tissues * (width // groups)].reshape(tissues, width // groups)
     )
     features = stream[None]
     input_grad = upstream.astype(jnp.bfloat16)[None]

time: 503 us -> 244 us (0.49)
  waiting for transfers between devices: 242 us -> 66.7 us
  local copies, waits for them, and re-layouts: 82.7 us -> 28.2 us
  blocking collectives: 69.4 us -> 43.4 us
    unnamed x10 -> x1, waiting for transfers between devices: 107 us -> 0.02 us
    psum x1 -> x0, blocking collectives: 69.4 us -> none  [per_device(): lax.psum((mix_local, donor_part, accept_part, kernel_local, embed_part, t...]
    scatter x2 -> x0, local copies, waits for them, and re-layouts: 51.2 us -> none  [the longest x1 29.5 us: per_device(): back_buffer = jnp.zeros((count, capacity, accept_back.shape[1]), jnp.bflo...]
    psum x1 -> x0, waiting for transfers between devices: 51 us -> none  [per_device(): lax.psum((mix_local, donor_part, accept_part, kernel_local, embed_part, t...]
    reduce_scatter x3 -> x1, waiting for transfers between devices: 65.2 us -> 40.7 us  [per_device(): lax.psum_scatter(pair_sum, 'dp', scatter_dimension=0, tiled=True)]
    all_gather x0 -> x1, blocking collectives: none -> 23.5 us  [per_device(): gathered = lax.all_gather(own_sum, 'seq', axis=0, tiled=False)]
    all_to_all x0 -> x1, blocking collectives: none -> 19.9 us  [per_device(): lax.all_to_all(blocks, 'seq', split_axis=0, concat_axis=0, tiled=True)]
    scatter-add x2 -> x0, other arithmetic: 8.48 us -> none  [the longest x1 5.29 us: per_device(): upstream.at[asked_rows]]
  transfers between devices with their start and end apart: 18 -> 13, of which waited for: 12 -> 8; matrix products, arithmetic and copies ran while one was open for 17% -> 5% of each run, Pallas kernels for 0% -> 0%
where the time goes in v1:
time: 244 us; the launch traced here: 243 us
  waiting for transfers between devices  66.7 us (27%)
  blocking collectives  43.4 us (18%)
  starting transfers between devices  42.6 us (17%)
  local copies, waits for them, and re-layouts  28.2 us (12%)
  matrix products  24.1 us (10%)
  other arithmetic  23.2 us (10%)
  between operations  14.9 us (6%)
    reduce_scatter x1, waiting for transfers between devices, per_device(): lax.psum_scatter(pair_sum, 'dp', scatter_dimension=0, tiled=True)  40.7 us
    all_gather x1, blocking collectives, per_device(): gathered = lax.all_gather(own_sum, 'seq', axis=0, tiled=False)  23.5 us
    all_to_all x1, blocking collectives, per_device(): lax.all_to_all(blocks, 'seq', split_axis=0, concat_axis=0, tiled=True)  19.9 us
    unnamed x71, local copies, waits for them, and re-layouts  13.7 us
    all_to_all x1, starting transfers between devices, per_device(): lax.all_to_all(answer, 'seq', split_axis=0, concat_axis=0, tiled=True)  10.6 us
    ppermute x4, waiting for transfers between devices, padded(): lax.ppermute(head, axis, [((i + 1) % count, i) for i in range(ends)])  10.1 us
    ppermute x4, starting transfers between devices, padded(): lax.ppermute(tail, axis, [(i, (i + 1) % count) for i in range(ends)])  9.67 us
    ppermute x4, starting transfers between devices, padded(): lax.ppermute(head, axis, [((i + 1) % count, i) for i in range(ends)])  9.11 us
  transfers between devices with their start and end apart: 13, of which 8 were waited for; matrix products, arithmetic and copies ran while one was open for 5% of the time, Pallas kernels for 0%

profile of v1, /device:TPU:1, one launch (start us, length us, event | category | flops | bytes accessed | tf_op | source)
XLA Modules:
  0.0 243.1 jit_solution(16650283508814399867)
XLA Ops:
  11.7 8.6 %all-to-all-start = ((s32[32,1,16]{2,1,0:T(1,128)}), s32[32,1,16]{2,1,0:T(1,128)S(1)}, u32[]{:S(2)}, u32[]{:S(2)}) async-start(s32[32,1,16]{2,1,0:T(1,128)} %bitcast.11), calls=%async_computation | async-start | bytes 32768 | tf_op jit(solution)/shard_map/all_to_all | solution.py:102
  22.7 3.5 %collective-permute-start = (bf16[16,768]{1,0:T(8,128)(2,1)S(1)}, bf16[16,768]{1,0:T(8,128)(2,1)S(1)}, u32[]{:S(2)}, u32[]{:S(2)}) collective-permute-start(bf16[16,768]{1,0:T(8,128)(2,1)S(1)} %get-tuple-element.78), channel_id=1, source_target_pairs={{0,1},{1,2},{2,3},{3,4},{4,5},{5,6},{6,7},{7,8},{8,9},{9,10},{10,1... | collective-permute-start | bytes 73736 | tf_op jit(solution)/shard_map/ppermute | solution.py:21
  26.2 1.9 collective-permute-start.1
  29.7 1.7 collective-permute-done.1
  35.8 2.0 collective-permute-start.2
  37.8 2.3 collective-permute-start.3
  40.4 4.4 %collective-permute-done.3 = bf16[128,768]{1,0:T(8,128)(2,1)S(1)} collective-permute-done((bf16[128,768]{1,0:T(8,128)(2,1)S(1)}, bf16[128,768]{1,0:T(8,128)(2,1)S(1)}, u32[]{:S(2)}, u32[]{:S(2)}) %collective-permute-start.3) | collective-permute-done | bytes 196640 | tf_op jit(solution)/shard_map/ppermute | solution.py:23
  48.6 2.7 %gather_fusion.1 = bf16[512,768]{1,0:T(8,128)(2,1)} fusion(bf16[512,768]{1,0:T(8,128)(2,1)S(1)} %fusion.31, s32[1024]{0:T(1024)S(1)} %pad_clamp_fusion), kind=kCustom, calls=%fused_computation.1 | custom fusion | bytes 1574912 | tf_op jit(solution)/shard_map/gather | solution.py:105
  51.4 2.2 fusion.40
  53.6 10.6 %all-to-all-start.1 = ((bf16[32,16,256]{2,1,0:T(8,128)(2,1)}), bf16[32,16,256]{2,1,0:T(8,128)(2,1)S(1)}, u32[]{:S(2)}, u32[]{:S(2)}) async-start(bf16[32,16,256]{2,1,0:T(8,128)(2,1)} %bitcast.13), calls=%async_computation.1 | async-start | bytes 524288 | tf_op jit(solution)/shard_map/all_to_all | solution.py:110
  66.7 6.3 %all-to-all-done.1 = bf16[32,16,256]{2,1,0:T(8,128)(2,1)S(1)} async-done(((bf16[32,16,256]{2,1,0:T(8,128)(2,1)}), bf16[32,16,256]{2,1,0:T(8,128)(2,1)S(1)}, u32[]{:S(2)}, u32[]{:S(2)}) %all-to-all-start.1) | async-done | bytes 262176 | tf_op jit(solution)/shard_map/all_to_all | solution.py:110
  77.3 4.4 %all-to-all-start.2 = ((bf16[32,16,256]{2,1,0:T(8,128)(2,1)}), bf16[32,16,256]{2,1,0:T(8,128)(2,1)}, u32[]{:S(2)}, u32[]{:S(2)}) async-start(bf16[32,16,256]{2,1,0:T(8,128)(2,1)} %bitcast.96), calls=%async_computation.2 | async-start | bytes 524288 | tf_op jit(solution)/shard_map/all_to_all | solution.py:134
  82.3 2.9 %fusion.64 = f32[512,768]{1,0:T(8,128)} fusion(f32[256,768]{1,0:T(8,128)S(1)} %fusion.99, s32[256]{0:T(256)} %bitcast.109), kind=kOutput, calls=%fused_computation.107 | convolution fusion | flops 1208090624 | bytes 2360320 | tf_op jit(solution)/shard_map/dot_general | solution.py:141
  85.1 5.5 %all-to-all-done.2 = bf16[32,16,256]{2,1,0:T(8,128)(2,1)} async-done(((bf16[32,16,256]{2,1,0:T(8,128)(2,1)}), bf16[32,16,256]{2,1,0:T(8,128)(2,1)}, u32[]{:S(2)}, u32[]{:S(2)}) %all-to-all-start.2) | async-done | bytes 262176 | tf_op jit(solution)/shard_map/all_to_all | solution.py:134
  92.2 1.9 convolution_add_fusion
  97.0 2.2 collective-permute-start.4
  99.2 2.1 collective-permute-start.5
  102.4 4.0 %collective-permute-done.5 = bf16[128,768]{1,0:T(8,128)(2,1)S(1)} collective-permute-done((bf16[128,768]{1,0:T(8,128)(2,1)}, bf16[128,768]{1,0:T(8,128)(2,1)S(1)}, u32[]{:S(2)}, u32[]{:S(2)}) %collective-permute-start.5) | collective-permute-done | bytes 196640 | tf_op jit(solution)/shard_map/ppermute | solution.py:23
  113.8 1.9 collective-permute-start.6
  115.8 2.8 %collective-permute-start.7 = (bf16[16,768]{1,0:T(8,128)(2,1)S(1)}, bf16[16,768]{1,0:T(8,128)(2,1)S(1)}, u32[]{:S(2)}, u32[]{:S(2)}) collective-permute-start(bf16[16,768]{1,0:T(8,128)(2,1)S(1)} %get-tuple-element.73), channel_id=1, source_target_pairs={{1,0},{2,1},{3,2},{4,3},{5,4},{6,5},{7,6},{8,7},{9,8},{10,9},{11,1... | collective-permute-start | bytes 73736 | tf_op jit(solution)/shard_map/ppermute | solution.py:23
  121.3 1.7 copy-done.12
  123.1 2.1 multiply_reduce_fusion.5
  125.4 3.2 %convert_bitcast_fusion = (bf16[1,512,768]{2,1,0:T(8,128)(2,1)}, f32[512,768]{1,0:T(8,128)S(1)}) fusion(f32[512,768]{1,0:T(8,128)} %copy-done.8, f32[512,768]{1,0:T(8,128)} %get-tuple-element.71, f32[512]{0:T(512)S(1)} %broadcast_multiply_fusion, bf16[512,768]{1,0:T(8,128)(2,1)S(1)} %copy-done.7, f32[512]{0:T(512)S(1)} %add_rsqrt_fusion.1), kind=kLoop, calls=%fused_computation.98 | loop fusion | flops 2752512 | bytes 6295552 | tf_op jit(solution)/shard_map/broadcast_in_dim | solution.py:245
  130.1 1.6 constant_dynamic-slice_fusion
  131.8 3.8 %collective-permute-done.8 = bf16[768,1152]{0,1:T(8,128)(2,1)} collective-permute-done((bf16[768,1152]{0,1:T(8,128)(2,1)S(1)}, bf16[768,1152]{0,1:T(8,128)(2,1)}, u32[]{:S(2)}, u32[]{:S(2)}) %collective-permute-start.8) | collective-permute-done | bytes 1769504 | tf_op jit(solution)/shard_map/ppermute | solution.py:219
  135.6 2.4 %add_convert_fusion = bf16[768,1152]{0,1:T(8,128)(2,1)S(1)} fusion(bf16[768,1152]{0,1:T(8,128)(2,1)} %collective-permute-done.8, bf16[768,2304]{0,1:T(8,128)(2,1)} %fusion.67, s32[]{:T(128)S(6)} %select_n.64), kind=kLoop, calls=%fused_computation.2 | loop fusion | flops 3538944 | bytes 5308420 | tf_op jit(solution)/shard_map/convert_element_type | solution.py:220
  138.0 2.2 copy.58
  140.3 40.7 %reduce-scatter.4.cloned.1.call-done = bf16[96,1152]{1,0:T(8,128)(2,1)} async-done(((bf16[768,1152]{1,0:T(8,128)(2,1)}), bf16[96,1152]{1,0:T(8,128)(2,1)}) %reduce-scatter.4.cloned.1.call-update) | async-done | bytes 221200 | tf_op jit(solution)/shard_map/reduce_scatter | solution.py:221
  182.9 1.9 reduce.26
  185.0 19.9 %all_to_all.32 = bf16[32,2,1728]{2,1,0:T(2,128)(2,1)S(1)} all-to-all(bf16[32,2,1728]{2,1,0:T(2,128)(2,1)S(1)} %reshape.297), channel_id=1, replica_groups=mesh['dp'=8,'seq'=32] {'seq'}, dimensions={0} | all-to-all | bytes 442368 | tf_op jit(solution)/shard_map/all_to_all | solution.py:224
  206.8 23.5 %all-gather.1 = bf16[32,2,3456]{2,1,0:T(2,128)(2,1)S(1)} all-gather(bf16[1,2,3456]{2,1,0:T(2,128)(2,1)S(1)} %bitcast.100), channel_id=2, replica_groups=mesh['dp'=8,'seq'=32] {'seq'}, dimensions={0}, use_global_device_ids=true | all-gather | bytes 456192 | tf_op jit(solution)/shard_map/all_gather | solution.py:227
  230.3 1.9 slice_reduce_fusion.1
  (173 shorter events, 49.3 us)
Async XLA Ops:
  7.2 44.2 %copy-start = (bf16[768,256]{1,0:T(8,128)(2,1)S(1)}, bf16[768,256]{1,0:T(8,128)(2,1)}, u32[]{:S(2)}) copy-start(bf16[768,256]{1,0:T(8,128)(2,1)} %param.17) | copy-start | bytes 1179652
  7.2 21.0 %copy-start.26 = (s32[1,256]{1,0:T(1,128)S(1)}, s32[1,256]{1,0:T(1,128)}, u32[]{:S(2)}) copy-start(s32[1,256]{1,0:T(1,128)} %param.20) | copy-start | bytes 3076
  7.2 21.0 %copy-start.23 = (bf16[2,3,768]{2,0,1:T(2,128)(2,1)S(1)}, bf16[2,3,768]{2,0,1:T(2,128)(2,1)}, u32[]{:S(2)}) copy-start(bf16[2,3,768]{2,0,1:T(2,128)(2,1)} %param.15) | copy-start | bytes 27652
  11.7 16.6 %all-to-all-start = ((s32[32,1,16]{2,1,0:T(1,128)}), s32[32,1,16]{2,1,0:T(1,128)S(1)}, u32[]{:S(2)}, u32[]{:S(2)}) async-start(s32[32,1,16]{2,1,0:T(1,128)} %bitcast.11), calls=%async_computation | async-start | bytes 32768 | tf_op jit(solution)/shard_map/all_to_all | solution.py:102
  21.5 11.4 %copy-start.6 = (bf16[512,768]{1,0:T(8,128)(2,1)}, bf16[512,768]{1,0:T(8,128)(2,1)S(1)}, u32[]{:S(2)}) copy-start(bf16[512,768]{1,0:T(8,128)(2,1)S(1)} %get-tuple-element.85) | copy-start | bytes 2359300
  22.7 7.0 %collective-permute-start = (bf16[16,768]{1,0:T(8,128)(2,1)S(1)}, bf16[16,768]{1,0:T(8,128)(2,1)S(1)}, u32[]{:S(2)}, u32[]{:S(2)}) collective-permute-start(bf16[16,768]{1,0:T(8,128)(2,1)S(1)} %get-tuple-element.78), channel_id=1, source_target_pairs={{0,1},{1,2},{2,3},{3,4},{4,5},{5,6},{6,7},{7,8},{8,9},{9,10},{10,1... | collective-permute-start | bytes 73736 | tf_op jit(solution)/shard_map/ppermute | solution.py:21
  26.2 5.1 %collective-permute-start.1 = (bf16[16,768]{1,0:T(8,128)(2,1)S(1)}, bf16[16,768]{1,0:T(8,128)(2,1)S(1)}, u32[]{:S(2)}, u32[]{:S(2)}) collective-permute-start(bf16[16,768]{1,0:T(8,128)(2,1)S(1)} %get-tuple-element.79), channel_id=1, source_target_pairs={{1,0},{2,1},{3,2},{4,3},{5,4},{6,5},{7,6},{8,7},{9,8},{10,9},{11,1... | collective-permute-start | bytes 73736 | tf_op jit(solution)/shard_map/ppermute | solution.py:23
  35.5 9.7 %copy-start.4 = (bf16[512,768]{1,0:T(8,128)(2,1)}, bf16[512,768]{1,0:T(8,128)(2,1)S(1)}, u32[]{:S(2)}) copy-start(bf16[512,768]{1,0:T(8,128)(2,1)S(1)} %get-tuple-element.87) | copy-start | bytes 2359300
  35.8 4.6 %collective-permute-start.2 = (bf16[128,768]{1,0:T(8,128)(2,1)S(1)}, bf16[128,768]{1,0:T(8,128)(2,1)S(1)}, u32[]{:S(2)}, u32[]{:S(2)}) collective-permute-start(bf16[128,768]{1,0:T(8,128)(2,1)S(1)} %get-tuple-element.76), channel_id=1, source_target_pairs={{0,1},{1,2},{2,3},{3,4},{4,5},{5,6},{6,7},{7,8},{8,9},{9,10},{10,1... | collective-permute-start | bytes 589832 | tf_op jit(solution)/shard_map/ppermute | solution.py:21
  37.8 7.0 %collective-permute-start.3 = (bf16[128,768]{1,0:T(8,128)(2,1)S(1)}, bf16[128,768]{1,0:T(8,128)(2,1)S(1)}, u32[]{:S(2)}, u32[]{:S(2)}) collective-permute-start(bf16[128,768]{1,0:T(8,128)(2,1)S(1)} %get-tuple-element.77), channel_id=1, source_target_pairs={{1,0},{2,1},{3,2},{4,3},{5,4},{6,5},{7,6},{8,7},{9,8},{10,9},{11,1... | collective-permute-start | bytes 589832 | tf_op jit(solution)/shard_map/ppermute | solution.py:23
  40.1 11.2 %copy-start.28 = (pred[512]{0:T(512)(128)(4,1)}, pred[512]{0:T(512)(128)(4,1)S(1)}, u32[]{:S(2)}) copy-start(pred[512]{0:T(512)(128)(4,1)S(1)} %broadcast_compare_fusion) | copy-start | bytes 1540
  48.6 15.6 %copy-start.1 = (bf16[512,768]{1,0:T(8,128)(2,1)}, bf16[512,768]{1,0:T(8,128)(2,1)S(1)}, u32[]{:S(2)}) copy-start(bf16[512,768]{1,0:T(8,128)(2,1)S(1)} %fusion.31) | copy-start | bytes 2359300
  53.6 19.5 %all-to-all-start.1 = ((bf16[32,16,256]{2,1,0:T(8,128)(2,1)}), bf16[32,16,256]{2,1,0:T(8,128)(2,1)S(1)}, u32[]{:S(2)}, u32[]{:S(2)}) async-start(bf16[32,16,256]{2,1,0:T(8,128)(2,1)} %bitcast.13), calls=%async_computation.1 | async-start | bytes 524288 | tf_op jit(solution)/shard_map/all_to_all | solution.py:110
  65.4 9.7 %copy-start.24 = (f32[4,256]{1,0:T(4,128)S(1)}, f32[4,256]{1,0:T(4,128)}, u32[]{:S(2)}) copy-start(f32[4,256]{1,0:T(4,128)} %param.18) | copy-start | bytes 12292
  65.4 9.7 %copy-start.25 = (s32[1,256]{1,0:T(1,128)S(1)}, s32[1,256]{1,0:T(1,128)}, u32[]{:S(2)}) copy-start(s32[1,256]{1,0:T(1,128)} %param.22) | copy-start | bytes 3076
  73.7 8.2 %copy-start.20 = (bf16[768,256]{1,0:T(8,128)(2,1)S(1)}, bf16[768,256]{1,0:T(8,128)(2,1)}, u32[]{:S(2)}) copy-start(bf16[768,256]{1,0:T(8,128)(2,1)} %param.16) | copy-start | bytes 1179652
  77.3 13.4 %all-to-all-start.2 = ((bf16[32,16,256]{2,1,0:T(8,128)(2,1)}), bf16[32,16,256]{2,1,0:T(8,128)(2,1)}, u32[]{:S(2)}, u32[]{:S(2)}) async-start(bf16[32,16,256]{2,1,0:T(8,128)(2,1)} %bitcast.96), calls=%async_computation.2 | async-start | bytes 524288 | tf_op jit(solution)/shard_map/all_to_all | solution.py:134
  81.7 99.2 %reduce-scatter.4.cloned.1.call-start = ((), (), s32[]{:S(2)}) async-start(), calls=%async_computation.5 | async-start | bytes 1990656 | tf_op jit(solution)/shard_map/reduce_scatter | solution.py:221
  85.1 7.0 %copy-start.29 = (pred[512]{0:T(512)(128)(4,1)S(1)}, pred[512]{0:T(512)(128)(4,1)}, u32[]{:S(2)}) copy-start(pred[512]{0:T(512)(128)(4,1)} %copy-done.28) | copy-start | bytes 1540
  92.2 1.9 copy-start.18
  92.2 2.1 copy-start.31
  97.0 5.4 %collective-permute-start.4 = (bf16[128,768]{1,0:T(8,128)(2,1)}, bf16[128,768]{1,0:T(8,128)(2,1)S(1)}, u32[]{:S(2)}, u32[]{:S(2)}) collective-permute-start(bf16[128,768]{1,0:T(8,128)(2,1)} %get-tuple-element.74), channel_id=1, source_target_pairs={{0,1},{1,2},{2,3},{3,4},{4,5},{5,6},{6,7},{7,8},{8,9},{9,10},{10,1... | collective-permute-start | bytes 589832 | tf_op jit(solution)/shard_map/ppermute | solution.py:21
  99.2 7.2 %collective-permute-start.5 = (bf16[128,768]{1,0:T(8,128)(2,1)}, bf16[128,768]{1,0:T(8,128)(2,1)S(1)}, u32[]{:S(2)}, u32[]{:S(2)}) collective-permute-start(bf16[128,768]{1,0:T(8,128)(2,1)} %get-tuple-element.75), channel_id=1, source_target_pairs={{1,0},{2,1},{3,2},{4,3},{5,4},{6,5},{7,6},{8,7},{9,8},{10,9},{11,1... | collective-permute-start | bytes 589832 | tf_op jit(solution)/shard_map/ppermute | solution.py:23
  102.3 5.4 %copy-start.3 = (f32[768,768]{1,0:T(8,128)S(1)}, f32[768,768]{1,0:T(8,128)}, u32[]{:S(2)}) copy-start(f32[768,768]{1,0:T(8,128)} %copy-done.2) | copy-start | bytes 7077892
  102.3 5.4 %copy-start.5 = (bf16[512,768]{1,0:T(8,128)(2,1)S(1)}, bf16[512,768]{1,0:T(8,128)(2,1)}, u32[]{:S(2)}) copy-start(bf16[512,768]{1,0:T(8,128)(2,1)} %copy-done.4) | copy-start | bytes 2359300
  109.1 2.1 copy-start.32
  112.8 5.7 %copy-start.19 = (f32[512,768]{1,0:T(8,128)S(1)}, f32[512,768]{1,0:T(8,128)}, u32[]{:S(2)}) copy-start(f32[512,768]{1,0:T(8,128)} %copy-done.17) | copy-start | bytes 4718596
  113.8 7.4 %collective-permute-start.6 = (bf16[16,768]{1,0:T(8,128)(2,1)S(1)}, bf16[16,768]{1,0:T(8,128)(2,1)S(1)}, u32[]{:S(2)}, u32[]{:S(2)}) collective-permute-start(bf16[16,768]{1,0:T(8,128)(2,1)S(1)} %get-tuple-element.72), channel_id=1, source_target_pairs={{0,1},{1,2},{2,3},{3,4},{4,5},{5,6},{6,7},{7,8},{8,9},{9,10},{10,1... | collective-permute-start | bytes 73736 | tf_op jit(solution)/shard_map/ppermute | solution.py:21
  115.8 4.1 %copy-start.22 = (bf16[512,768]{1,0:T(8,128)(2,1)S(1)}, bf16[512,768]{1,0:T(8,128)(2,1)}, u32[]{:S(2)}) copy-start(bf16[512,768]{1,0:T(8,128)(2,1)} %gather_fusion.1) | copy-start | bytes 2359300
  115.8 7.2 %collective-permute-start.7 = (bf16[16,768]{1,0:T(8,128)(2,1)S(1)}, bf16[16,768]{1,0:T(8,128)(2,1)S(1)}, u32[]{:S(2)}, u32[]{:S(2)}) collective-permute-start(bf16[16,768]{1,0:T(8,128)(2,1)S(1)} %get-tuple-element.73), channel_id=1, source_target_pairs={{1,0},{2,1},{3,2},{4,3},{5,4},{6,5},{7,6},{8,7},{9,8},{10,9},{11,1... | collective-permute-start | bytes 73736 | tf_op jit(solution)/shard_map/ppermute | solution.py:23
  125.4 3.2 %copy-start.27 = (s32[1,512]{1,0:T(1,128)S(1)}, s32[1,512]{1,0:T(1,128)}, u32[]{:S(2)}) copy-start(s32[1,512]{1,0:T(1,128)} %param.12) | copy-start | bytes 6148
  131.6 3.9 %collective-permute-start.8 = (bf16[768,1152]{0,1:T(8,128)(2,1)S(1)}, bf16[768,1152]{0,1:T(8,128)(2,1)}, u32[]{:S(2)}, u32[]{:S(2)}) collective-permute-start(bf16[768,1152]{0,1:T(8,128)(2,1)S(1)} %constant_dynamic-slice_fusion), channel_id=1, source_target_pairs={{0,1},{1,0},{2,3},{3,2},{4,5},{5,4},{6,7},{7,6},{8,9},{9,8},{10,11... | collective-permute-start | bytes 5308424 | tf_op jit(solution)/shard_map/ppermute | solution.py:219
  (14 other events, 19.2 us)
Sparse Core Ops, SparseCore 0:
  140.4 40.4 reduce-scatter.3

commit v2 on v1

--- a/solution.py
+++ b/solution.py
@@ -220,11 +220,14 @@
     pair_sum = (own.astype(jnp.float32) + partner.astype(jnp.float32)).astype(jnp.bfloat16)
     scattered = lax.psum_scatter(pair_sum, "dp", scatter_dimension=0, tiled=True)
     share = rows // count
-    blocks = scattered.reshape(count, share * half)
+    tiles = share * half // lanes
+    blocks = scattered.reshape(count, tiles, lanes)
     exchanged = lax.all_to_all(blocks, "seq", split_axis=0, concat_axis=0, tiled=True)
-    by_core = exchanged.astype(jnp.float32).reshape(count // 2, 2, share * half)
-    own_sum = jnp.sum(by_core, axis=0).astype(jnp.bfloat16)
-    gathered = lax.all_gather(own_sum, "seq", axis=0, tiled=False)
+    by_core = exchanged.astype(jnp.float32).reshape(count // 2, 2, tiles, lanes)
+    own_sum = jnp.sum(by_core, axis=0).astype(jnp.bfloat16).reshape(2 * tiles, lanes)
+    gathered = lax.all_gather(own_sum, "seq", axis=0, tiled=False).reshape(
+        count, 2, share * half
+    )
     summed = jnp.concatenate(
         [gathered[:, 0].reshape(rows, half), gathered[:, 1].reshape(rows, half)], axis=1
     ).astype(jnp.float32)

time: 244 us -> 240 us (0.984)
  other arithmetic: 23.2 us -> 19.8 us
    all_to_all x2 -> x0, other arithmetic: 3.21 us -> none  [per_device(): lax.all_to_all(blocks, 'seq', split_axis=0, concat_axis=0, tiled=True)]
    unnamed x71 -> x69, local copies, waits for them, and re-layouts: 13.7 us -> 13.2 us
where the time goes in v2:
time: 240 us; the launch traced here: 239 us
  waiting for transfers between devices  66.8 us (28%)
  blocking collectives  43.3 us (18%)
  starting transfers between devices  42.6 us (18%)
  local copies, waits for them, and re-layouts  27.1 us (11%)
  matrix products  24 us (10%)
  other arithmetic  19.8 us (8%)
  between operations  14.9 us (6%)
    reduce_scatter x1, waiting for transfers between devices, per_device(): lax.psum_scatter(pair_sum, 'dp', scatter_dimension=0, tiled=True)  40.8 us
    all_gather x1, blocking collectives, per_device(): lax.all_gather(own_sum, 'seq', axis=0, tiled=False)  23.1 us
    all_to_all x1, blocking collectives, per_device(): lax.all_to_all(blocks, 'seq', split_axis=0, concat_axis=0, tiled=True)  20.1 us
    unnamed x69, local copies, waits for them, and re-layouts  13.2 us
    all_to_all x1, starting transfers between devices, per_device(): lax.all_to_all(answer, 'seq', split_axis=0, concat_axis=0, tiled=True)  10.6 us
    ppermute x4, waiting for transfers between devices, padded(): lax.ppermute(head, axis, [((i + 1) % count, i) for i in range(ends)])  10.1 us
    ppermute x4, starting transfers between devices, padded(): lax.ppermute(tail, axis, [(i, (i + 1) % count) for i in range(ends)])  9.67 us
    ppermute x4, starting transfers between devices, padded(): lax.ppermute(head, axis, [((i + 1) % count, i) for i in range(ends)])  9.11 us
  transfers between devices with their start and end apart: 13, of which 8 were waited for; matrix products, arithmetic and copies ran while one was open for 5% of the time, Pallas kernels for 0%

profile of v2, /device:TPU:1, one launch (start us, length us, event | category | flops | bytes accessed | tf_op | source)
XLA Modules:
  0.0 238.5 jit_solution(15658869962210309964)
XLA Ops:
  11.7 8.6 %all-to-all-start = ((s32[32,1,16]{2,1,0:T(1,128)}), s32[32,1,16]{2,1,0:T(1,128)S(1)}, u32[]{:S(2)}, u32[]{:S(2)}) async-start(s32[32,1,16]{2,1,0:T(1,128)} %bitcast.11), calls=%async_computation | async-start | bytes 32768 | tf_op jit(solution)/shard_map/all_to_all | solution.py:102
  22.7 3.5 %collective-permute-start = (bf16[16,768]{1,0:T(8,128)(2,1)S(1)}, bf16[16,768]{1,0:T(8,128)(2,1)S(1)}, u32[]{:S(2)}, u32[]{:S(2)}) collective-permute-start(bf16[16,768]{1,0:T(8,128)(2,1)S(1)} %get-tuple-element.78), channel_id=1, source_target_pairs={{0,1},{1,2},{2,3},{3,4},{4,5},{5,6},{6,7},{7,8},{8,9},{9,10},{10,1... | collective-permute-start | bytes 73736 | tf_op jit(solution)/shard_map/ppermute | solution.py:21
  26.2 1.9 collective-permute-start.1
  29.7 1.7 collective-permute-done.1
  35.8 2.0 collective-permute-start.2
  37.8 2.3 collective-permute-start.3
  40.4 4.4 %collective-permute-done.3 = bf16[128,768]{1,0:T(8,128)(2,1)S(1)} collective-permute-done((bf16[128,768]{1,0:T(8,128)(2,1)S(1)}, bf16[128,768]{1,0:T(8,128)(2,1)S(1)}, u32[]{:S(2)}, u32[]{:S(2)}) %collective-permute-start.3) | collective-permute-done | bytes 196640 | tf_op jit(solution)/shard_map/ppermute | solution.py:23
  48.6 2.7 %gather_fusion.1 = bf16[512,768]{1,0:T(8,128)(2,1)} fusion(bf16[512,768]{1,0:T(8,128)(2,1)S(1)} %fusion.31, s32[1024]{0:T(1024)S(1)} %pad_clamp_fusion), kind=kCustom, calls=%fused_computation.1 | custom fusion | bytes 1574912 | tf_op jit(solution)/shard_map/gather | solution.py:105
  51.4 2.2 fusion.40
  53.6 10.6 %all-to-all-start.1 = ((bf16[32,16,256]{2,1,0:T(8,128)(2,1)}), bf16[32,16,256]{2,1,0:T(8,128)(2,1)S(1)}, u32[]{:S(2)}, u32[]{:S(2)}) async-start(bf16[32,16,256]{2,1,0:T(8,128)(2,1)} %bitcast.13), calls=%async_computation.1 | async-start | bytes 524288 | tf_op jit(solution)/shard_map/all_to_all | solution.py:110
  66.7 6.3 %all-to-all-done.1 = bf16[32,16,256]{2,1,0:T(8,128)(2,1)S(1)} async-done(((bf16[32,16,256]{2,1,0:T(8,128)(2,1)}), bf16[32,16,256]{2,1,0:T(8,128)(2,1)S(1)}, u32[]{:S(2)}, u32[]{:S(2)}) %all-to-all-start.1) | async-done | bytes 262176 | tf_op jit(solution)/shard_map/all_to_all | solution.py:110
  77.3 4.4 %all-to-all-start.2 = ((bf16[32,16,256]{2,1,0:T(8,128)(2,1)}), bf16[32,16,256]{2,1,0:T(8,128)(2,1)}, u32[]{:S(2)}, u32[]{:S(2)}) async-start(bf16[32,16,256]{2,1,0:T(8,128)(2,1)} %bitcast.96), calls=%async_computation.2 | async-start | bytes 524288 | tf_op jit(solution)/shard_map/all_to_all | solution.py:134
  82.3 2.9 %fusion.64 = f32[512,768]{1,0:T(8,128)} fusion(f32[256,768]{1,0:T(8,128)S(1)} %fusion.99, s32[256]{0:T(256)} %bitcast.109), kind=kOutput, calls=%fused_computation.107 | convolution fusion | flops 1208090624 | bytes 2360320 | tf_op jit(solution)/shard_map/dot_general | solution.py:141
  85.1 5.5 %all-to-all-done.2 = bf16[32,16,256]{2,1,0:T(8,128)(2,1)} async-done(((bf16[32,16,256]{2,1,0:T(8,128)(2,1)}), bf16[32,16,256]{2,1,0:T(8,128)(2,1)}, u32[]{:S(2)}, u32[]{:S(2)}) %all-to-all-start.2) | async-done | bytes 262176 | tf_op jit(solution)/shard_map/all_to_all | solution.py:134
  92.2 1.9 convolution_add_fusion
  94.3 1.5 fusion.27
  97.0 2.2 collective-permute-start.4
  99.2 2.1 collective-permute-start.5
  102.4 4.0 %collective-permute-done.5 = bf16[128,768]{1,0:T(8,128)(2,1)S(1)} collective-permute-done((bf16[128,768]{1,0:T(8,128)(2,1)}, bf16[128,768]{1,0:T(8,128)(2,1)S(1)}, u32[]{:S(2)}, u32[]{:S(2)}) %collective-permute-start.5) | collective-permute-done | bytes 196640 | tf_op jit(solution)/shard_map/ppermute | solution.py:23
  113.9 1.9 collective-permute-start.6
  115.8 2.8 %collective-permute-start.7 = (bf16[16,768]{1,0:T(8,128)(2,1)S(1)}, bf16[16,768]{1,0:T(8,128)(2,1)S(1)}, u32[]{:S(2)}, u32[]{:S(2)}) collective-permute-start(bf16[16,768]{1,0:T(8,128)(2,1)S(1)} %get-tuple-element.73), channel_id=1, source_target_pairs={{1,0},{2,1},{3,2},{4,3},{5,4},{6,5},{7,6},{8,7},{9,8},{10,9},{11,1... | collective-permute-start | bytes 73736 | tf_op jit(solution)/shard_map/ppermute | solution.py:23
  121.3 1.7 copy-done.12
  123.1 2.1 multiply_reduce_fusion.5
  125.4 3.2 %convert_bitcast_fusion = (bf16[1,512,768]{2,1,0:T(8,128)(2,1)}, f32[512,768]{1,0:T(8,128)S(1)}) fusion(f32[512,768]{1,0:T(8,128)} %copy-done.8, f32[512,768]{1,0:T(8,128)} %get-tuple-element.71, f32[512]{0:T(512)S(1)} %broadcast_multiply_fusion, bf16[512,768]{1,0:T(8,128)(2,1)S(1)} %copy-done.7, f32[512]{0:T(512)S(1)} %add_rsqrt_fusion.1), kind=kLoop, calls=%fused_computation.98 | loop fusion | flops 2752512 | bytes 6295552 | tf_op jit(solution)/shard_map/broadcast_in_dim | solution.py:248
  130.1 1.6 constant_dynamic-slice_fusion
  131.8 3.8 %collective-permute-done.8 = bf16[768,1152]{0,1:T(8,128)(2,1)} collective-permute-done((bf16[768,1152]{0,1:T(8,128)(2,1)S(1)}, bf16[768,1152]{0,1:T(8,128)(2,1)}, u32[]{:S(2)}, u32[]{:S(2)}) %collective-permute-start.8) | collective-permute-done | bytes 1769504 | tf_op jit(solution)/shard_map/ppermute | solution.py:219
  135.6 2.4 %add_convert_fusion = bf16[768,1152]{0,1:T(8,128)(2,1)S(1)} fusion(bf16[768,1152]{0,1:T(8,128)(2,1)} %collective-permute-done.8, bf16[768,2304]{0,1:T(8,128)(2,1)} %fusion.67, s32[]{:T(128)S(6)} %select_n.64), kind=kLoop, calls=%fused_computation.2 | loop fusion | flops 3538944 | bytes 5308420 | tf_op jit(solution)/shard_map/convert_element_type | solution.py:220
  138.0 2.2 copy.56
  140.3 40.8 %reduce-scatter.4.cloned.1.call-done = bf16[96,1152]{1,0:T(8,128)(2,1)} async-done(((bf16[768,1152]{1,0:T(8,128)(2,1)}), bf16[96,1152]{1,0:T(8,128)(2,1)}) %reduce-scatter.4.cloned.1.call-update) | async-done | bytes 221200 | tf_op jit(solution)/shard_map/reduce_scatter | solution.py:221
  182.3 20.1 %all_to_all.27 = bf16[32,27,128]{2,1,0:T(8,128)(2,1)S(1)} all-to-all(bf16[32,27,128]{2,1,0:T(8,128)(2,1)S(1)} %reshape.257), channel_id=1, replica_groups=mesh['dp'=8,'seq'=32] {'seq'}, dimensions={0} | all-to-all | bytes 442368 | tf_op jit(solution)/shard_map/all_to_all | solution.py:225
  202.5 23.1 %all_gather.3 = bf16[32,54,128]{2,1,0:T(8,128)(2,1)S(1)} all-gather(bf16[1,54,128]{2,1,0:T(8,128)(2,1)S(1)} %convert_element_type.168), channel_id=1, replica_groups=mesh['dp'=8,'seq'=32] {'seq'}, dimensions={0}, use_global_device_ids=true | all-gather | bytes 456192 | tf_op jit(solution)/shard_map/all_gather | solution.py:228
  225.7 1.9 slice_reduce_fusion.1
  (169 shorter events, 45.2 us)
Async XLA Ops:
  7.2 44.2 %copy-start = (bf16[768,256]{1,0:T(8,128)(2,1)S(1)}, bf16[768,256]{1,0:T(8,128)(2,1)}, u32[]{:S(2)}) copy-start(bf16[768,256]{1,0:T(8,128)(2,1)} %param.17) | copy-start | bytes 1179652
  7.2 21.0 %copy-start.26 = (s32[1,256]{1,0:T(1,128)S(1)}, s32[1,256]{1,0:T(1,128)}, u32[]{:S(2)}) copy-start(s32[1,256]{1,0:T(1,128)} %param.20) | copy-start | bytes 3076
  7.2 21.0 %copy-start.23 = (bf16[2,3,768]{2,0,1:T(2,128)(2,1)S(1)}, bf16[2,3,768]{2,0,1:T(2,128)(2,1)}, u32[]{:S(2)}) copy-start(bf16[2,3,768]{2,0,1:T(2,128)(2,1)} %param.15) | copy-start | bytes 27652
  11.7 16.6 %all-to-all-start = ((s32[32,1,16]{2,1,0:T(1,128)}), s32[32,1,16]{2,1,0:T(1,128)S(1)}, u32[]{:S(2)}, u32[]{:S(2)}) async-start(s32[32,1,16]{2,1,0:T(1,128)} %bitcast.11), calls=%async_computation | async-start | bytes 32768 | tf_op jit(solution)/shard_map/all_to_all | solution.py:102
  21.5 11.4 %copy-start.6 = (bf16[512,768]{1,0:T(8,128)(2,1)}, bf16[512,768]{1,0:T(8,128)(2,1)S(1)}, u32[]{:S(2)}) copy-start(bf16[512,768]{1,0:T(8,128)(2,1)S(1)} %get-tuple-element.85) | copy-start | bytes 2359300
  22.7 7.0 %collective-permute-start = (bf16[16,768]{1,0:T(8,128)(2,1)S(1)}, bf16[16,768]{1,0:T(8,128)(2,1)S(1)}, u32[]{:S(2)}, u32[]{:S(2)}) collective-permute-start(bf16[16,768]{1,0:T(8,128)(2,1)S(1)} %get-tuple-element.78), channel_id=1, source_target_pairs={{0,1},{1,2},{2,3},{3,4},{4,5},{5,6},{6,7},{7,8},{8,9},{9,10},{10,1... | collective-permute-start | bytes 73736 | tf_op jit(solution)/shard_map/ppermute | solution.py:21
  26.2 5.1 %collective-permute-start.1 = (bf16[16,768]{1,0:T(8,128)(2,1)S(1)}, bf16[16,768]{1,0:T(8,128)(2,1)S(1)}, u32[]{:S(2)}, u32[]{:S(2)}) collective-permute-start(bf16[16,768]{1,0:T(8,128)(2,1)S(1)} %get-tuple-element.79), channel_id=1, source_target_pairs={{1,0},{2,1},{3,2},{4,3},{5,4},{6,5},{7,6},{8,7},{9,8},{10,9},{11,1... | collective-permute-start | bytes 73736 | tf_op jit(solution)/shard_map/ppermute | solution.py:23
  35.5 9.7 %copy-start.4 = (bf16[512,768]{1,0:T(8,128)(2,1)}, bf16[512,768]{1,0:T(8,128)(2,1)S(1)}, u32[]{:S(2)}) copy-start(bf16[512,768]{1,0:T(8,128)(2,1)S(1)} %get-tuple-element.87) | copy-start | bytes 2359300
  35.8 4.6 %collective-permute-start.2 = (bf16[128,768]{1,0:T(8,128)(2,1)S(1)}, bf16[128,768]{1,0:T(8,128)(2,1)S(1)}, u32[]{:S(2)}, u32[]{:S(2)}) collective-permute-start(bf16[128,768]{1,0:T(8,128)(2,1)S(1)} %get-tuple-element.76), channel_id=1, source_target_pairs={{0,1},{1,2},{2,3},{3,4},{4,5},{5,6},{6,7},{7,8},{8,9},{9,10},{10,1... | collective-permute-start | bytes 589832 | tf_op jit(solution)/shard_map/ppermute | solution.py:21
  37.8 7.0 %collective-permute-start.3 = (bf16[128,768]{1,0:T(8,128)(2,1)S(1)}, bf16[128,768]{1,0:T(8,128)(2,1)S(1)}, u32[]{:S(2)}, u32[]{:S(2)}) collective-permute-start(bf16[128,768]{1,0:T(8,128)(2,1)S(1)} %get-tuple-element.77), channel_id=1, source_target_pairs={{1,0},{2,1},{3,2},{4,3},{5,4},{6,5},{7,6},{8,7},{9,8},{10,9},{11,1... | collective-permute-start | bytes 589832 | tf_op jit(solution)/shard_map/ppermute | solution.py:23
  40.1 11.2 %copy-start.28 = (pred[512]{0:T(512)(128)(4,1)}, pred[512]{0:T(512)(128)(4,1)S(1)}, u32[]{:S(2)}) copy-start(pred[512]{0:T(512)(128)(4,1)S(1)} %broadcast_compare_fusion) | copy-start | bytes 1540
  48.6 15.6 %copy-start.1 = (bf16[512,768]{1,0:T(8,128)(2,1)}, bf16[512,768]{1,0:T(8,128)(2,1)S(1)}, u32[]{:S(2)}) copy-start(bf16[512,768]{1,0:T(8,128)(2,1)S(1)} %fusion.31) | copy-start | bytes 2359300
  53.6 19.5 %all-to-all-start.1 = ((bf16[32,16,256]{2,1,0:T(8,128)(2,1)}), bf16[32,16,256]{2,1,0:T(8,128)(2,1)S(1)}, u32[]{:S(2)}, u32[]{:S(2)}) async-start(bf16[32,16,256]{2,1,0:T(8,128)(2,1)} %bitcast.13), calls=%async_computation.1 | async-start | bytes 524288 | tf_op jit(solution)/shard_map/all_to_all | solution.py:110
  65.4 9.7 %copy-start.24 = (f32[4,256]{1,0:T(4,128)S(1)}, f32[4,256]{1,0:T(4,128)}, u32[]{:S(2)}) copy-start(f32[4,256]{1,0:T(4,128)} %param.18) | copy-start | bytes 12292
  65.4 9.7 %copy-start.25 = (s32[1,256]{1,0:T(1,128)S(1)}, s32[1,256]{1,0:T(1,128)}, u32[]{:S(2)}) copy-start(s32[1,256]{1,0:T(1,128)} %param.22) | copy-start | bytes 3076
  73.7 8.2 %copy-start.20 = (bf16[768,256]{1,0:T(8,128)(2,1)S(1)}, bf16[768,256]{1,0:T(8,128)(2,1)}, u32[]{:S(2)}) copy-start(bf16[768,256]{1,0:T(8,128)(2,1)} %param.16) | copy-start | bytes 1179652
  77.3 13.4 %all-to-all-start.2 = ((bf16[32,16,256]{2,1,0:T(8,128)(2,1)}), bf16[32,16,256]{2,1,0:T(8,128)(2,1)}, u32[]{:S(2)}, u32[]{:S(2)}) async-start(bf16[32,16,256]{2,1,0:T(8,128)(2,1)} %bitcast.96), calls=%async_computation.2 | async-start | bytes 524288 | tf_op jit(solution)/shard_map/all_to_all | solution.py:134
  81.7 99.3 %reduce-scatter.4.cloned.1.call-start = ((), (), s32[]{:S(2)}) async-start(), calls=%async_computation.5 | async-start | bytes 1990656 | tf_op jit(solution)/shard_map/reduce_scatter | solution.py:221
  85.1 7.0 %copy-start.29 = (pred[512]{0:T(512)(128)(4,1)S(1)}, pred[512]{0:T(512)(128)(4,1)}, u32[]{:S(2)}) copy-start(pred[512]{0:T(512)(128)(4,1)} %copy-done.28) | copy-start | bytes 1540
  92.2 1.9 copy-start.18
  92.2 2.1 copy-start.31
  97.0 5.4 %collective-permute-start.4 = (bf16[128,768]{1,0:T(8,128)(2,1)}, bf16[128,768]{1,0:T(8,128)(2,1)S(1)}, u32[]{:S(2)}, u32[]{:S(2)}) collective-permute-start(bf16[128,768]{1,0:T(8,128)(2,1)} %get-tuple-element.74), channel_id=1, source_target_pairs={{0,1},{1,2},{2,3},{3,4},{4,5},{5,6},{6,7},{7,8},{8,9},{9,10},{10,1... | collective-permute-start | bytes 589832 | tf_op jit(solution)/shard_map/ppermute | solution.py:21
  99.2 7.2 %collective-permute-start.5 = (bf16[128,768]{1,0:T(8,128)(2,1)}, bf16[128,768]{1,0:T(8,128)(2,1)S(1)}, u32[]{:S(2)}, u32[]{:S(2)}) collective-permute-start(bf16[128,768]{1,0:T(8,128)(2,1)} %get-tuple-element.75), channel_id=1, source_target_pairs={{1,0},{2,1},{3,2},{4,3},{5,4},{6,5},{7,6},{8,7},{9,8},{10,9},{11,1... | collective-permute-start | bytes 589832 | tf_op jit(solution)/shard_map/ppermute | solution.py:23
  102.4 5.4 %copy-start.3 = (f32[768,768]{1,0:T(8,128)S(1)}, f32[768,768]{1,0:T(8,128)}, u32[]{:S(2)}) copy-start(f32[768,768]{1,0:T(8,128)} %copy-done.2) | copy-start | bytes 7077892
  102.4 5.4 %copy-start.5 = (bf16[512,768]{1,0:T(8,128)(2,1)S(1)}, bf16[512,768]{1,0:T(8,128)(2,1)}, u32[]{:S(2)}) copy-start(bf16[512,768]{1,0:T(8,128)(2,1)} %copy-done.4) | copy-start | bytes 2359300
  109.2 2.1 copy-start.32
  112.8 5.7 %copy-start.19 = (f32[512,768]{1,0:T(8,128)S(1)}, f32[512,768]{1,0:T(8,128)}, u32[]{:S(2)}) copy-start(f32[512,768]{1,0:T(8,128)} %copy-done.17) | copy-start | bytes 4718596
  113.9 7.4 %collective-permute-start.6 = (bf16[16,768]{1,0:T(8,128)(2,1)S(1)}, bf16[16,768]{1,0:T(8,128)(2,1)S(1)}, u32[]{:S(2)}, u32[]{:S(2)}) collective-permute-start(bf16[16,768]{1,0:T(8,128)(2,1)S(1)} %get-tuple-element.72), channel_id=1, source_target_pairs={{0,1},{1,2},{2,3},{3,4},{4,5},{5,6},{6,7},{7,8},{8,9},{9,10},{10,1... | collective-permute-start | bytes 73736 | tf_op jit(solution)/shard_map/ppermute | solution.py:21
  115.8 4.1 %copy-start.22 = (bf16[512,768]{1,0:T(8,128)(2,1)S(1)}, bf16[512,768]{1,0:T(8,128)(2,1)}, u32[]{:S(2)}) copy-start(bf16[512,768]{1,0:T(8,128)(2,1)} %gather_fusion.1) | copy-start | bytes 2359300
  115.8 7.2 %collective-permute-start.7 = (bf16[16,768]{1,0:T(8,128)(2,1)S(1)}, bf16[16,768]{1,0:T(8,128)(2,1)S(1)}, u32[]{:S(2)}, u32[]{:S(2)}) collective-permute-start(bf16[16,768]{1,0:T(8,128)(2,1)S(1)} %get-tuple-element.73), channel_id=1, source_target_pairs={{1,0},{2,1},{3,2},{4,3},{5,4},{6,5},{7,6},{8,7},{9,8},{10,9},{11,1... | collective-permute-start | bytes 73736 | tf_op jit(solution)/shard_map/ppermute | solution.py:23
  125.4 3.2 %copy-start.27 = (s32[1,512]{1,0:T(1,128)S(1)}, s32[1,512]{1,0:T(1,128)}, u32[]{:S(2)}) copy-start(s32[1,512]{1,0:T(1,128)} %param.12) | copy-start | bytes 6148
  131.7 3.9 %collective-permute-start.8 = (bf16[768,1152]{0,1:T(8,128)(2,1)S(1)}, bf16[768,1152]{0,1:T(8,128)(2,1)}, u32[]{:S(2)}, u32[]{:S(2)}) collective-permute-start(bf16[768,1152]{0,1:T(8,128)(2,1)S(1)} %constant_dynamic-slice_fusion), channel_id=1, source_target_pairs={{0,1},{1,0},{2,3},{3,2},{4,5},{5,4},{6,7},{7,6},{8,9},{9,8},{10,11... | collective-permute-start | bytes 5308424 | tf_op jit(solution)/shard_map/ppermute | solution.py:219
  (14 other events, 19.2 us)
Sparse Core Ops, SparseCore 0:
  140.4 40.5 reduce-scatter.3

commit v3 on v2

--- a/solution.py
+++ b/solution.py
@@ -225,9 +225,13 @@
     exchanged = lax.all_to_all(blocks, "seq", split_axis=0, concat_axis=0, tiled=True)
     by_core = exchanged.astype(jnp.float32).reshape(count // 2, 2, tiles, lanes)
     own_sum = jnp.sum(by_core, axis=0).astype(jnp.bfloat16).reshape(2 * tiles, lanes)
-    gathered = lax.all_gather(own_sum, "seq", axis=0, tiled=False).reshape(
-        count, 2, share * half
-    )
+    gathered = lax.all_to_all(
+        jnp.broadcast_to(own_sum[None], (count,) + own_sum.shape),
+        "seq",
+        split_axis=0,
+        concat_axis=0,
+        tiled=True,
+    ).reshape(count, 2, share * half)
     summed = jnp.concatenate(
         [gathered[:, 0].reshape(rows, half), gathered[:, 1].reshape(rows, half)], axis=1
     ).astype(jnp.float32)

time: 240 us -> 231 us (0.963)
  blocking collectives: 43.3 us -> 34.5 us
    all_gather x1 -> x0, blocking collectives: 23.1 us -> none  [per_device(): lax.all_gather(own_sum, 'seq', axis=0, tiled=False)]
    all_to_all x0 -> x1, blocking collectives: none -> 14.3 us  [per_device(): lax.all_to_all(jnp.broadcast_to(own_sum[None], (count,) + own_sum.shape),...]
where the time goes in v3:
time: 231 us; the launch traced here: 230 us
  waiting for transfers between devices  66.8 us (29%)
  starting transfers between devices  42.6 us (18%)
  blocking collectives  34.5 us (15%)
  local copies, waits for them, and re-layouts  27.2 us (12%)
  matrix products  24 us (10%)
  other arithmetic  19.8 us (9%)
  between operations  14.9 us (6%)
    reduce_scatter x1, waiting for transfers between devices, per_device(): lax.psum_scatter(pair_sum, 'dp', scatter_dimension=0, tiled=True)  40.8 us
    all_to_all x1, blocking collectives, per_device(): lax.all_to_all(blocks, 'seq', split_axis=0, concat_axis=0, tiled=True)  20.1 us
    all_to_all x1, blocking collectives, per_device(): lax.all_to_all(jnp.broadcast_to(own_sum[None], (count,) + own_sum.shape),...  14.3 us
    unnamed x69, local copies, waits for them, and re-layouts  13.2 us
    all_to_all x1, starting transfers between devices, per_device(): lax.all_to_all(answer, 'seq', split_axis=0, concat_axis=0, tiled=True)  10.6 us
    ppermute x4, waiting for transfers between devices, padded(): lax.ppermute(head, axis, [((i + 1) % count, i) for i in range(ends)])  10.1 us
    ppermute x4, starting transfers between devices, padded(): lax.ppermute(tail, axis, [(i, (i + 1) % count) for i in range(ends)])  9.67 us
    ppermute x4, starting transfers between devices, padded(): lax.ppermute(head, axis, [((i + 1) % count, i) for i in range(ends)])  9.11 us
  transfers between devices with their start and end apart: 13, of which 8 were waited for; matrix products, arithmetic and copies ran while one was open for 5% of the time, Pallas kernels for 0%

profile of v3, /device:TPU:1, one launch (start us, length us, event | category | flops | bytes accessed | tf_op | source)
XLA Modules:
  0.0 229.8 jit_solution(16329604003715021538)
XLA Ops:
  11.7 8.6 %all-to-all-start = ((s32[32,1,16]{2,1,0:T(1,128)}), s32[32,1,16]{2,1,0:T(1,128)S(1)}, u32[]{:S(2)}, u32[]{:S(2)}) async-start(s32[32,1,16]{2,1,0:T(1,128)} %bitcast.11), calls=%async_computation | async-start | bytes 32768 | tf_op jit(solution)/shard_map/all_to_all | solution.py:102
  22.7 3.5 %collective-permute-start = (bf16[16,768]{1,0:T(8,128)(2,1)S(1)}, bf16[16,768]{1,0:T(8,128)(2,1)S(1)}, u32[]{:S(2)}, u32[]{:S(2)}) collective-permute-start(bf16[16,768]{1,0:T(8,128)(2,1)S(1)} %get-tuple-element.78), channel_id=1, source_target_pairs={{0,1},{1,2},{2,3},{3,4},{4,5},{5,6},{6,7},{7,8},{8,9},{9,10},{10,1... | collective-permute-start | bytes 73736 | tf_op jit(solution)/shard_map/ppermute | solution.py:21
  26.2 1.9 collective-permute-start.1
  29.7 1.7 collective-permute-done.1
  35.8 2.0 collective-permute-start.2
  37.8 2.3 %collective-permute-start.3 = (bf16[128,768]{1,0:T(8,128)(2,1)S(1)}, bf16[128,768]{1,0:T(8,128)(2,1)S(1)}, u32[]{:S(2)}, u32[]{:S(2)}) collective-permute-start(bf16[128,768]{1,0:T(8,128)(2,1)S(1)} %get-tuple-element.77), channel_id=1, source_target_pairs={{1,0},{2,1},{3,2},{4,3},{5,4},{6,5},{7,6},{8,7},{9,8},{10,9},{11,1... | collective-permute-start | bytes 589832 | tf_op jit(solution)/shard_map/ppermute | solution.py:23
  40.4 4.4 %collective-permute-done.3 = bf16[128,768]{1,0:T(8,128)(2,1)S(1)} collective-permute-done((bf16[128,768]{1,0:T(8,128)(2,1)S(1)}, bf16[128,768]{1,0:T(8,128)(2,1)S(1)}, u32[]{:S(2)}, u32[]{:S(2)}) %collective-permute-start.3) | collective-permute-done | bytes 196640 | tf_op jit(solution)/shard_map/ppermute | solution.py:23
  48.6 2.7 %gather_fusion.1 = bf16[512,768]{1,0:T(8,128)(2,1)} fusion(bf16[512,768]{1,0:T(8,128)(2,1)S(1)} %fusion.31, s32[1024]{0:T(1024)S(1)} %pad_clamp_fusion), kind=kCustom, calls=%fused_computation.1 | custom fusion | bytes 1574912 | tf_op jit(solution)/shard_map/gather | solution.py:105
  51.4 2.2 fusion.40
  53.6 10.6 %all-to-all-start.1 = ((bf16[32,16,256]{2,1,0:T(8,128)(2,1)}), bf16[32,16,256]{2,1,0:T(8,128)(2,1)S(1)}, u32[]{:S(2)}, u32[]{:S(2)}) async-start(bf16[32,16,256]{2,1,0:T(8,128)(2,1)} %bitcast.13), calls=%async_computation.1 | async-start | bytes 524288 | tf_op jit(solution)/shard_map/all_to_all | solution.py:110
  66.7 6.3 %all-to-all-done.1 = bf16[32,16,256]{2,1,0:T(8,128)(2,1)S(1)} async-done(((bf16[32,16,256]{2,1,0:T(8,128)(2,1)}), bf16[32,16,256]{2,1,0:T(8,128)(2,1)S(1)}, u32[]{:S(2)}, u32[]{:S(2)}) %all-to-all-start.1) | async-done | bytes 262176 | tf_op jit(solution)/shard_map/all_to_all | solution.py:110
  77.3 4.4 %all-to-all-start.2 = ((bf16[32,16,256]{2,1,0:T(8,128)(2,1)}), bf16[32,16,256]{2,1,0:T(8,128)(2,1)}, u32[]{:S(2)}, u32[]{:S(2)}) async-start(bf16[32,16,256]{2,1,0:T(8,128)(2,1)} %bitcast.96), calls=%async_computation.2 | async-start | bytes 524288 | tf_op jit(solution)/shard_map/all_to_all | solution.py:134
  82.3 2.9 %fusion.64 = f32[512,768]{1,0:T(8,128)} fusion(f32[256,768]{1,0:T(8,128)S(1)} %fusion.99, s32[256]{0:T(256)} %bitcast.109), kind=kOutput, calls=%fused_computation.107 | convolution fusion | flops 1208090624 | bytes 2360320 | tf_op jit(solution)/shard_map/dot_general | solution.py:141
  85.1 5.5 %all-to-all-done.2 = bf16[32,16,256]{2,1,0:T(8,128)(2,1)} async-done(((bf16[32,16,256]{2,1,0:T(8,128)(2,1)}), bf16[32,16,256]{2,1,0:T(8,128)(2,1)}, u32[]{:S(2)}, u32[]{:S(2)}) %all-to-all-start.2) | async-done | bytes 262176 | tf_op jit(solution)/shard_map/all_to_all | solution.py:134
  92.2 1.9 convolution_add_fusion
  94.3 1.5 fusion.27
  97.0 2.2 collective-permute-start.4
  99.2 2.1 collective-permute-start.5
  102.4 4.0 %collective-permute-done.5 = bf16[128,768]{1,0:T(8,128)(2,1)S(1)} collective-permute-done((bf16[128,768]{1,0:T(8,128)(2,1)}, bf16[128,768]{1,0:T(8,128)(2,1)S(1)}, u32[]{:S(2)}, u32[]{:S(2)}) %collective-permute-start.5) | collective-permute-done | bytes 196640 | tf_op jit(solution)/shard_map/ppermute | solution.py:23
  113.9 1.9 collective-permute-start.6
  115.8 2.8 %collective-permute-start.7 = (bf16[16,768]{1,0:T(8,128)(2,1)S(1)}, bf16[16,768]{1,0:T(8,128)(2,1)S(1)}, u32[]{:S(2)}, u32[]{:S(2)}) collective-permute-start(bf16[16,768]{1,0:T(8,128)(2,1)S(1)} %get-tuple-element.73), channel_id=1, source_target_pairs={{1,0},{2,1},{3,2},{4,3},{5,4},{6,5},{7,6},{8,7},{9,8},{10,9},{11,1... | collective-permute-start | bytes 73736 | tf_op jit(solution)/shard_map/ppermute | solution.py:23
  121.3 1.7 copy-done.12
  123.1 2.1 multiply_reduce_fusion.5
  125.4 3.2 %convert_bitcast_fusion = (bf16[1,512,768]{2,1,0:T(8,128)(2,1)}, f32[512,768]{1,0:T(8,128)S(1)}) fusion(f32[512,768]{1,0:T(8,128)} %copy-done.8, f32[512,768]{1,0:T(8,128)} %get-tuple-element.71, f32[512]{0:T(512)S(1)} %broadcast_multiply_fusion, bf16[512,768]{1,0:T(8,128)(2,1)S(1)} %copy-done.7, f32[512]{0:T(512)S(1)} %add_rsqrt_fusion.1), kind=kLoop, calls=%fused_computation.98 | loop fusion | flops 2752512 | bytes 6295552 | tf_op jit(solution)/shard_map/broadcast_in_dim | solution.py:252
  130.1 1.6 constant_dynamic-slice_fusion
  131.8 3.8 %collective-permute-done.8 = bf16[768,1152]{0,1:T(8,128)(2,1)} collective-permute-done((bf16[768,1152]{0,1:T(8,128)(2,1)S(1)}, bf16[768,1152]{0,1:T(8,128)(2,1)}, u32[]{:S(2)}, u32[]{:S(2)}) %collective-permute-start.8) | collective-permute-done | bytes 1769504 | tf_op jit(solution)/shard_map/ppermute | solution.py:219
  135.6 2.4 %add_convert_fusion = bf16[768,1152]{0,1:T(8,128)(2,1)S(1)} fusion(bf16[768,1152]{0,1:T(8,128)(2,1)} %collective-permute-done.8, bf16[768,2304]{0,1:T(8,128)(2,1)} %fusion.67, s32[]{:T(128)S(6)} %select_n.64), kind=kLoop, calls=%fused_computation.2 | loop fusion | flops 3538944 | bytes 5308420 | tf_op jit(solution)/shard_map/convert_element_type | solution.py:220
  138.0 2.2 copy.56
  140.3 40.8 %reduce-scatter.4.cloned.1.call-done = bf16[96,1152]{1,0:T(8,128)(2,1)} async-done(((bf16[768,1152]{1,0:T(8,128)(2,1)}), bf16[96,1152]{1,0:T(8,128)(2,1)}) %reduce-scatter.4.cloned.1.call-update) | async-done | bytes 221200 | tf_op jit(solution)/shard_map/reduce_scatter | solution.py:221
  182.3 20.1 %all_to_all.32 = bf16[32,27,128]{2,1,0:T(8,128)(2,1)S(1)} all-to-all(bf16[32,27,128]{2,1,0:T(8,128)(2,1)S(1)} %reshape.252), channel_id=1, replica_groups=mesh['dp'=8,'seq'=32] {'seq'}, dimensions={0} | all-to-all | bytes 442368 | tf_op jit(solution)/shard_map/all_to_all | solution.py:225
  202.5 14.3 %all_to_all.33 = bf16[32,54,128]{2,1,0:T(8,128)(2,1)S(1)} all-to-all(bf16[32,54,128]{2,1,0:T(8,128)(2,1)S(1)} %broadcast_in_dim.38), channel_id=1, replica_groups=mesh['dp'=8,'seq'=32] {'seq'}, dimensions={0} | all-to-all | bytes 884736 | tf_op jit(solution)/shard_map/all_to_all | solution.py:228
  217.0 1.9 slice_reduce_fusion.1
  (170 shorter events, 45.2 us)
Async XLA Ops:
  7.2 44.2 %copy-start = (bf16[768,256]{1,0:T(8,128)(2,1)S(1)}, bf16[768,256]{1,0:T(8,128)(2,1)}, u32[]{:S(2)}) copy-start(bf16[768,256]{1,0:T(8,128)(2,1)} %param.17) | copy-start | bytes 1179652
  7.2 21.0 %copy-start.26 = (s32[1,256]{1,0:T(1,128)S(1)}, s32[1,256]{1,0:T(1,128)}, u32[]{:S(2)}) copy-start(s32[1,256]{1,0:T(1,128)} %param.20) | copy-start | bytes 3076
  7.2 21.0 %copy-start.23 = (bf16[2,3,768]{2,0,1:T(2,128)(2,1)S(1)}, bf16[2,3,768]{2,0,1:T(2,128)(2,1)}, u32[]{:S(2)}) copy-start(bf16[2,3,768]{2,0,1:T(2,128)(2,1)} %param.15) | copy-start | bytes 27652
  11.7 16.6 %all-to-all-start = ((s32[32,1,16]{2,1,0:T(1,128)}), s32[32,1,16]{2,1,0:T(1,128)S(1)}, u32[]{:S(2)}, u32[]{:S(2)}) async-start(s32[32,1,16]{2,1,0:T(1,128)} %bitcast.11), calls=%async_computation | async-start | bytes 32768 | tf_op jit(solution)/shard_map/all_to_all | solution.py:102
  21.5 11.4 %copy-start.6 = (bf16[512,768]{1,0:T(8,128)(2,1)}, bf16[512,768]{1,0:T(8,128)(2,1)S(1)}, u32[]{:S(2)}) copy-start(bf16[512,768]{1,0:T(8,128)(2,1)S(1)} %get-tuple-element.85) | copy-start | bytes 2359300
  22.7 7.0 %collective-permute-start = (bf16[16,768]{1,0:T(8,128)(2,1)S(1)}, bf16[16,768]{1,0:T(8,128)(2,1)S(1)}, u32[]{:S(2)}, u32[]{:S(2)}) collective-permute-start(bf16[16,768]{1,0:T(8,128)(2,1)S(1)} %get-tuple-element.78), channel_id=1, source_target_pairs={{0,1},{1,2},{2,3},{3,4},{4,5},{5,6},{6,7},{7,8},{8,9},{9,10},{10,1... | collective-permute-start | bytes 73736 | tf_op jit(solution)/shard_map/ppermute | solution.py:21
  26.2 5.1 %collective-permute-start.1 = (bf16[16,768]{1,0:T(8,128)(2,1)S(1)}, bf16[16,768]{1,0:T(8,128)(2,1)S(1)}, u32[]{:S(2)}, u32[]{:S(2)}) collective-permute-start(bf16[16,768]{1,0:T(8,128)(2,1)S(1)} %get-tuple-element.79), channel_id=1, source_target_pairs={{1,0},{2,1},{3,2},{4,3},{5,4},{6,5},{7,6},{8,7},{9,8},{10,9},{11,1... | collective-permute-start | bytes 73736 | tf_op jit(solution)/shard_map/ppermute | solution.py:23
  35.5 9.7 %copy-start.4 = (bf16[512,768]{1,0:T(8,128)(2,1)}, bf16[512,768]{1,0:T(8,128)(2,1)S(1)}, u32[]{:S(2)}) copy-start(bf16[512,768]{1,0:T(8,128)(2,1)S(1)} %get-tuple-element.87) | copy-start | bytes 2359300
  35.8 4.6 %collective-permute-start.2 = (bf16[128,768]{1,0:T(8,128)(2,1)S(1)}, bf16[128,768]{1,0:T(8,128)(2,1)S(1)}, u32[]{:S(2)}, u32[]{:S(2)}) collective-permute-start(bf16[128,768]{1,0:T(8,128)(2,1)S(1)} %get-tuple-element.76), channel_id=1, source_target_pairs={{0,1},{1,2},{2,3},{3,4},{4,5},{5,6},{6,7},{7,8},{8,9},{9,10},{10,1... | collective-permute-start | bytes 589832 | tf_op jit(solution)/shard_map/ppermute | solution.py:21
  37.8 7.0 %collective-permute-start.3 = (bf16[128,768]{1,0:T(8,128)(2,1)S(1)}, bf16[128,768]{1,0:T(8,128)(2,1)S(1)}, u32[]{:S(2)}, u32[]{:S(2)}) collective-permute-start(bf16[128,768]{1,0:T(8,128)(2,1)S(1)} %get-tuple-element.77), channel_id=1, source_target_pairs={{1,0},{2,1},{3,2},{4,3},{5,4},{6,5},{7,6},{8,7},{9,8},{10,9},{11,1... | collective-permute-start | bytes 589832 | tf_op jit(solution)/shard_map/ppermute | solution.py:23
  40.1 11.2 %copy-start.28 = (pred[512]{0:T(512)(128)(4,1)}, pred[512]{0:T(512)(128)(4,1)S(1)}, u32[]{:S(2)}) copy-start(pred[512]{0:T(512)(128)(4,1)S(1)} %broadcast_compare_fusion) | copy-start | bytes 1540
  48.6 15.6 %copy-start.1 = (bf16[512,768]{1,0:T(8,128)(2,1)}, bf16[512,768]{1,0:T(8,128)(2,1)S(1)}, u32[]{:S(2)}) copy-start(bf16[512,768]{1,0:T(8,128)(2,1)S(1)} %fusion.31) | copy-start | bytes 2359300
  53.6 19.5 %all-to-all-start.1 = ((bf16[32,16,256]{2,1,0:T(8,128)(2,1)}), bf16[32,16,256]{2,1,0:T(8,128)(2,1)S(1)}, u32[]{:S(2)}, u32[]{:S(2)}) async-start(bf16[32,16,256]{2,1,0:T(8,128)(2,1)} %bitcast.13), calls=%async_computation.1 | async-start | bytes 524288 | tf_op jit(solution)/shard_map/all_to_all | solution.py:110
  65.4 9.7 %copy-start.24 = (f32[4,256]{1,0:T(4,128)S(1)}, f32[4,256]{1,0:T(4,128)}, u32[]{:S(2)}) copy-start(f32[4,256]{1,0:T(4,128)} %param.18) | copy-start | bytes 12292
  65.4 9.7 %copy-start.25 = (s32[1,256]{1,0:T(1,128)S(1)}, s32[1,256]{1,0:T(1,128)}, u32[]{:S(2)}) copy-start(s32[1,256]{1,0:T(1,128)} %param.22) | copy-start | bytes 3076
  73.7 8.2 %copy-start.20 = (bf16[768,256]{1,0:T(8,128)(2,1)S(1)}, bf16[768,256]{1,0:T(8,128)(2,1)}, u32[]{:S(2)}) copy-start(bf16[768,256]{1,0:T(8,128)(2,1)} %param.16) | copy-start | bytes 1179652
  77.3 13.4 %all-to-all-start.2 = ((bf16[32,16,256]{2,1,0:T(8,128)(2,1)}), bf16[32,16,256]{2,1,0:T(8,128)(2,1)}, u32[]{:S(2)}, u32[]{:S(2)}) async-start(bf16[32,16,256]{2,1,0:T(8,128)(2,1)} %bitcast.96), calls=%async_computation.2 | async-start | bytes 524288 | tf_op jit(solution)/shard_map/all_to_all | solution.py:134
  81.7 99.3 %reduce-scatter.4.cloned.1.call-start = ((), (), s32[]{:S(2)}) async-start(), calls=%async_computation.6 | async-start | bytes 1990656 | tf_op jit(solution)/shard_map/reduce_scatter | solution.py:221
  85.1 7.0 %copy-start.29 = (pred[512]{0:T(512)(128)(4,1)S(1)}, pred[512]{0:T(512)(128)(4,1)}, u32[]{:S(2)}) copy-start(pred[512]{0:T(512)(128)(4,1)} %copy-done.28) | copy-start | bytes 1540
  92.2 1.9 copy-start.18
  92.2 2.1 copy-start.31
  97.0 5.4 %collective-permute-start.4 = (bf16[128,768]{1,0:T(8,128)(2,1)}, bf16[128,768]{1,0:T(8,128)(2,1)S(1)}, u32[]{:S(2)}, u32[]{:S(2)}) collective-permute-start(bf16[128,768]{1,0:T(8,128)(2,1)} %get-tuple-element.74), channel_id=1, source_target_pairs={{0,1},{1,2},{2,3},{3,4},{4,5},{5,6},{6,7},{7,8},{8,9},{9,10},{10,1... | collective-permute-start | bytes 589832 | tf_op jit(solution)/shard_map/ppermute | solution.py:21
  99.2 7.2 %collective-permute-start.5 = (bf16[128,768]{1,0:T(8,128)(2,1)}, bf16[128,768]{1,0:T(8,128)(2,1)S(1)}, u32[]{:S(2)}, u32[]{:S(2)}) collective-permute-start(bf16[128,768]{1,0:T(8,128)(2,1)} %get-tuple-element.75), channel_id=1, source_target_pairs={{1,0},{2,1},{3,2},{4,3},{5,4},{6,5},{7,6},{8,7},{9,8},{10,9},{11,1... | collective-permute-start | bytes 589832 | tf_op jit(solution)/shard_map/ppermute | solution.py:23
  102.4 5.4 %copy-start.3 = (f32[768,768]{1,0:T(8,128)S(1)}, f32[768,768]{1,0:T(8,128)}, u32[]{:S(2)}) copy-start(f32[768,768]{1,0:T(8,128)} %copy-done.2) | copy-start | bytes 7077892
  102.4 5.4 %copy-start.5 = (bf16[512,768]{1,0:T(8,128)(2,1)S(1)}, bf16[512,768]{1,0:T(8,128)(2,1)}, u32[]{:S(2)}) copy-start(bf16[512,768]{1,0:T(8,128)(2,1)} %copy-done.4) | copy-start | bytes 2359300
  109.2 2.1 copy-start.32
  112.8 5.7 %copy-start.19 = (f32[512,768]{1,0:T(8,128)S(1)}, f32[512,768]{1,0:T(8,128)}, u32[]{:S(2)}) copy-start(f32[512,768]{1,0:T(8,128)} %copy-done.17) | copy-start | bytes 4718596
  113.9 7.4 %collective-permute-start.6 = (bf16[16,768]{1,0:T(8,128)(2,1)S(1)}, bf16[16,768]{1,0:T(8,128)(2,1)S(1)}, u32[]{:S(2)}, u32[]{:S(2)}) collective-permute-start(bf16[16,768]{1,0:T(8,128)(2,1)S(1)} %get-tuple-element.72), channel_id=1, source_target_pairs={{0,1},{1,2},{2,3},{3,4},{4,5},{5,6},{6,7},{7,8},{8,9},{9,10},{10,1... | collective-permute-start | bytes 73736 | tf_op jit(solution)/shard_map/ppermute | solution.py:21
  115.8 4.1 %copy-start.22 = (bf16[512,768]{1,0:T(8,128)(2,1)S(1)}, bf16[512,768]{1,0:T(8,128)(2,1)}, u32[]{:S(2)}) copy-start(bf16[512,768]{1,0:T(8,128)(2,1)} %gather_fusion.1) | copy-start | bytes 2359300
  115.8 7.2 %collective-permute-start.7 = (bf16[16,768]{1,0:T(8,128)(2,1)S(1)}, bf16[16,768]{1,0:T(8,128)(2,1)S(1)}, u32[]{:S(2)}, u32[]{:S(2)}) collective-permute-start(bf16[16,768]{1,0:T(8,128)(2,1)S(1)} %get-tuple-element.73), channel_id=1, source_target_pairs={{1,0},{2,1},{3,2},{4,3},{5,4},{6,5},{7,6},{8,7},{9,8},{10,9},{11,1... | collective-permute-start | bytes 73736 | tf_op jit(solution)/shard_map/ppermute | solution.py:23
  125.4 3.2 %copy-start.27 = (s32[1,512]{1,0:T(1,128)S(1)}, s32[1,512]{1,0:T(1,128)}, u32[]{:S(2)}) copy-start(s32[1,512]{1,0:T(1,128)} %param.12) | copy-start | bytes 6148
  131.7 3.9 %collective-permute-start.8 = (bf16[768,1152]{0,1:T(8,128)(2,1)S(1)}, bf16[768,1152]{0,1:T(8,128)(2,1)}, u32[]{:S(2)}, u32[]{:S(2)}) collective-permute-start(bf16[768,1152]{0,1:T(8,128)(2,1)S(1)} %constant_dynamic-slice_fusion), channel_id=1, source_target_pairs={{0,1},{1,0},{2,3},{3,2},{4,5},{5,4},{6,7},{7,6},{8,9},{9,8},{10,11... | collective-permute-start | bytes 5308424 | tf_op jit(solution)/shard_map/ppermute | solution.py:219
  (14 other events, 19.2 us)
Sparse Core Ops, SparseCore 0:
  140.4 40.5 reduce-scatter.3

commit v4 on v3

--- a/solution.py
+++ b/solution.py
@@ -60,18 +60,35 @@
 ):
     length = tokens.shape[1]
     tok_row = tokens[0]
-    vocab_hits = tok_row[:, None] == jnp.arange(embed_table.shape[0], dtype=jnp.int32)[None, :]
-    stream = jnp.dot(
-        vocab_hits.astype(jnp.bfloat16), embed_table, preferred_element_type=jnp.float32
+    vocab = jnp.arange(embed_table.shape[0], dtype=jnp.int32)[None, :]
+    vocab_hits = tok_row[:, None] == vocab
+    first = FIRST_DILATION
+    tok_wide = padded(tok_row, (("seq", 0),), first)
+    wide_stream = jnp.dot(
+        (tok_wide[:, None] == vocab).astype(jnp.bfloat16),
+        embed_table,
+        preferred_element_type=jnp.float32,
     ).astype(jnp.bfloat16)
+    stream = wide_stream[first : first + length]
+    place = lax.axis_index("seq")
+    spots = jnp.arange(length + 2 * first, dtype=jnp.int32)
+    inside = ((spots >= first) | (place > 0)) & (
+        (spots < first + length) | (place < lax.axis_size("seq") - 1)
+    )
     dilation_sizes = (FIRST_DILATION, SECOND_DILATION)
     saved = []
     for layer_index in range(2):
         dilation = dilation_sizes[layer_index]
         stream_wide = stream.astype(jnp.float32)
-        normed, inv_rms = normalize(stream_wide)
-        norm_low = normed.astype(jnp.bfloat16)
-        padded_input = norm_halo(norm_low, dilation)
+        if layer_index == 0:
+            normed_all, inv_all = normalize(wide_stream.astype(jnp.float32))
+            normed = normed_all[first : first + length]
+            inv_rms = inv_all[first : first + length]
+            padded_input = jnp.where(inside[:, None], normed_all.astype(jnp.bfloat16), 0)
+        else:
+            normed, inv_rms = normalize(stream_wide)
+            norm_low = normed.astype(jnp.bfloat16)
+            padded_input = norm_halo(norm_low, dilation)
         padded_wide = padded_input.astype(jnp.float32)
         kernel_wide = kernels[layer_index].astype(jnp.float32)
         conv_out = (

time: 231 us -> 230 us (level)
  waiting for transfers between devices: 66.8 us -> 58.6 us
  starting transfers between devices: 42.6 us -> 47.5 us
  local copies, waits for them, and re-layouts: 27.2 us -> 30.5 us
    ppermute x4, waiting for transfers between devices: 10.1 us -> 0.89 us  [padded(): lax.ppermute(head, axis, [((i + 1) % count, i) for i in range(ends)])]
    ppermute x4, starting transfers between devices: 9.67 us -> 13.6 us  [padded(): lax.ppermute(tail, axis, [(i, (i + 1) % count) for i in range(ends)])]
    unnamed x69 -> x65, local copies, waits for them, and re-layouts: 13.2 us -> 14.9 us
  transfers between devices with their start and end apart: 13 -> 13, of which waited for: 8 -> 8; matrix products, arithmetic and copies ran while one was open for 5% -> 10% of each run, Pallas kernels for 0% -> 0%
where the time goes in v4:
time: 230 us; the launch traced here: 229 us
  waiting for transfers between devices  58.6 us (25%)
  starting transfers between devices  47.5 us (21%)
  blocking collectives  34.5 us (15%)
  local copies, waits for them, and re-layouts  30.5 us (13%)
  matrix products  23.5 us (10%)
  other arithmetic  19.7 us (9%)
  between operations  14.9 us (6%)
    reduce_scatter x1, waiting for transfers between devices, per_device(): lax.psum_scatter(pair_sum, 'dp', scatter_dimension=0, tiled=True)  40.1 us
    all_to_all x1, blocking collectives, per_device(): lax.all_to_all(blocks, 'seq', split_axis=0, concat_axis=0, tiled=True)  20.1 us
    unnamed x65, local copies, waits for them, and re-layouts  14.9 us
    all_to_all x1, blocking collectives, per_device(): lax.all_to_all(jnp.broadcast_to(own_sum[None], (count,) + own_sum.shape),...  14.3 us
    ppermute x4, starting transfers between devices, padded(): lax.ppermute(tail, axis, [(i, (i + 1) % count) for i in range(ends)])  13.6 us
    ppermute x4, starting transfers between devices, padded(): lax.ppermute(head, axis, [((i + 1) % count, i) for i in range(ends)])  11.2 us
    all_to_all x1, starting transfers between devices, per_device(): lax.all_to_all(answer, 'seq', split_axis=0, concat_axis=0, tiled=True)  10.3 us
    all_to_all x1, starting transfers between devices, per_device(): lax.all_to_all(request, 'seq', split_axis=0, concat_axis=0, tiled=True)  8.39 us
  transfers between devices with their start and end apart: 13, of which 8 were waited for; matrix products, arithmetic and copies ran while one was open for 10% of the time, Pallas kernels for 0%

profile of v4, /device:TPU:1, one launch (start us, length us, event | category | flops | bytes accessed | tf_op | source)
XLA Modules:
  0.0 229.1 jit_solution(18024370879637058451)
XLA Ops:
  8.0 5.1 %collective-permute-start.1 = (s32[16]{0:T(128)S(1)}, s32[16]{0:T(128)S(1)}, u32[]{:S(2)}, u32[]{:S(2)}) collective-permute-start(s32[16]{0:T(128)S(1)} %get-tuple-element.83), channel_id=1, source_target_pairs={{1,0},{2,1},{3,2},{4,3},{5,4},{6,5},{7,6},{8,7},{9,8},{10,9},{11,1... | collective-permute-start | bytes 200 | tf_op jit(solution)/shard_map/ppermute | solution.py:23
  13.1 1.9 collective-permute-start
  19.5 8.4 %all-to-all-start = ((s32[32,1,16]{2,1,0:T(1,128)}), s32[32,1,16]{2,1,0:T(1,128)S(1)}, u32[]{:S(2)}, u32[]{:S(2)}) async-start(s32[32,1,16]{2,1,0:T(1,128)} %bitcast.13), calls=%async_computation | async-start | bytes 32768 | tf_op jit(solution)/shard_map/all_to_all | solution.py:119
  31.5 1.5 convert_multiply_fusion.2
  33.5 1.4 copy-done.27
  38.1 2.1 collective-permute-start.3
  40.2 3.4 %collective-permute-start.2 = (bf16[128,768]{1,0:T(8,128)(2,1)S(1)}, bf16[128,768]{1,0:T(8,128)(2,1)S(1)}, u32[]{:S(2)}, u32[]{:S(2)}) collective-permute-start(bf16[128,768]{1,0:T(8,128)(2,1)S(1)} %get-tuple-element.76), channel_id=1, source_target_pairs={{0,1},{1,2},{2,3},{3,4},{4,5},{5,6},{6,7},{7,8},{8,9},{9,10},{10,1... | collective-permute-start | bytes 589832 | tf_op jit(solution)/shard_map/ppermute | solution.py:21
  52.0 2.7 %gather_fusion.1 = bf16[512,768]{1,0:T(8,128)(2,1)} fusion(bf16[512,768]{1,0:T(8,128)(2,1)S(1)} %fusion.23, s32[1024]{0:T(1024)S(1)} %pad_clamp_fusion), kind=kCustom, calls=%fused_computation.1 | custom fusion | bytes 1574912 | tf_op jit(solution)/shard_map/gather | solution.py:122
  54.7 2.2 fusion.32
  57.0 10.3 %all-to-all-start.1 = ((bf16[32,16,256]{2,1,0:T(8,128)(2,1)}), bf16[32,16,256]{2,1,0:T(8,128)(2,1)}, u32[]{:S(2)}, u32[]{:S(2)}) async-start(bf16[32,16,256]{2,1,0:T(8,128)(2,1)} %bitcast.15), calls=%async_computation.1 | async-start | bytes 524288 | tf_op jit(solution)/shard_map/all_to_all | solution.py:127
  68.5 1.3 fusion.91
  69.8 6.3 %all-to-all-done.1 = bf16[32,16,256]{2,1,0:T(8,128)(2,1)} async-done(((bf16[32,16,256]{2,1,0:T(8,128)(2,1)}), bf16[32,16,256]{2,1,0:T(8,128)(2,1)}, u32[]{:S(2)}, u32[]{:S(2)}) %all-to-all-start.1) | async-done | bytes 262176 | tf_op jit(solution)/shard_map/all_to_all | solution.py:127
  80.2 3.8 %all-to-all-start.2 = ((bf16[32,16,256]{2,1,0:T(8,128)(2,1)}), bf16[32,16,256]{2,1,0:T(8,128)(2,1)S(1)}, u32[]{:S(2)}, u32[]{:S(2)}) async-start(bf16[32,16,256]{2,1,0:T(8,128)(2,1)} %bitcast.102), calls=%async_computation.2 | async-start | bytes 524288 | tf_op jit(solution)/shard_map/all_to_all | solution.py:151
  84.2 3.4 %fusion.56 = f32[512,768]{1,0:T(8,128)} fusion(f32[256,768]{1,0:T(8,128)} %fusion.92, s32[256]{0:T(256)} %bitcast.116), kind=kOutput, calls=%fused_computation.101 | convolution fusion | flops 1208090624 | bytes 2360320 | tf_op jit(solution)/shard_map/dot_general | solution.py:158
  87.6 5.3 %all-to-all-done.2 = bf16[32,16,256]{2,1,0:T(8,128)(2,1)S(1)} async-done(((bf16[32,16,256]{2,1,0:T(8,128)(2,1)}), bf16[32,16,256]{2,1,0:T(8,128)(2,1)S(1)}, u32[]{:S(2)}, u32[]{:S(2)}) %all-to-all-start.2) | async-done | bytes 262176 | tf_op jit(solution)/shard_map/all_to_all | solution.py:151
  94.3 1.9 convolution_add_fusion
  96.5 1.5 fusion.21
  99.0 2.0 collective-permute-start.5
  101.1 3.5 %collective-permute-start.4 = (bf16[128,768]{1,0:T(8,128)(2,1)}, bf16[128,768]{1,0:T(8,128)(2,1)}, u32[]{:S(2)}, u32[]{:S(2)}) collective-permute-start(bf16[128,768]{1,0:T(8,128)(2,1)} %get-tuple-element.74), channel_id=1, source_target_pairs={{0,1},{1,2},{2,3},{3,4},{4,5},{5,6},{6,7},{7,8},{8,9},{9,10},{10,1... | collective-permute-start | bytes 589832 | tf_op jit(solution)/shard_map/ppermute | solution.py:21
  107.5 1.4 maximum_convert_fusion.1
  112.5 1.6 fusion.14
  115.1 1.9 collective-permute-start.7
  117.0 4.7 %collective-permute-start.6 = (bf16[16,768]{1,0:T(8,128)(2,1)S(1)}, bf16[16,768]{1,0:T(8,128)(2,1)S(1)}, u32[]{:S(2)}, u32[]{:S(2)}) collective-permute-start(bf16[16,768]{1,0:T(8,128)(2,1)S(1)} %get-tuple-element.72), channel_id=1, source_target_pairs={{0,1},{1,2},{2,3},{3,4},{4,5},{5,6},{6,7},{7,8},{8,9},{9,10},{10,1... | collective-permute-start | bytes 73736 | tf_op jit(solution)/shard_map/ppermute | solution.py:21
  123.6 1.7 copy-done.12
  130.0 1.6 constant_dynamic-slice_fusion
  131.7 3.8 %collective-permute-done.8 = bf16[768,1152]{0,1:T(8,128)(2,1)} collective-permute-done((bf16[768,1152]{0,1:T(8,128)(2,1)S(1)}, bf16[768,1152]{0,1:T(8,128)(2,1)}, u32[]{:S(2)}, u32[]{:S(2)}) %collective-permute-start.8) | collective-permute-done | bytes 1769504 | tf_op jit(solution)/shard_map/ppermute | solution.py:236
  135.5 2.4 %add_convert_fusion = bf16[768,1152]{0,1:T(8,128)(2,1)S(1)} fusion(bf16[768,1152]{0,1:T(8,128)(2,1)} %collective-permute-done.8, bf16[768,2304]{0,1:T(8,128)(2,1)} %fusion.59, s32[]{:T(128)S(6)} %select_n.69), kind=kLoop, calls=%fused_computation.2 | loop fusion | flops 3538944 | bytes 5308420 | tf_op jit(solution)/shard_map/convert_element_type | solution.py:237
  137.9 2.2 copy.56
  140.2 40.1 %reduce-scatter.4.cloned.1.call-done = bf16[96,1152]{1,0:T(8,128)(2,1)} async-done(((bf16[768,1152]{1,0:T(8,128)(2,1)}), bf16[96,1152]{1,0:T(8,128)(2,1)}) %reduce-scatter.4.cloned.1.call-update) | async-done | bytes 221200 | tf_op jit(solution)/shard_map/reduce_scatter | solution.py:238
  181.5 20.1 %all_to_all.32 = bf16[32,27,128]{2,1,0:T(8,128)(2,1)S(1)} all-to-all(bf16[32,27,128]{2,1,0:T(8,128)(2,1)S(1)} %reshape.279), channel_id=1, replica_groups=mesh['dp'=8,'seq'=32] {'seq'}, dimensions={0} | all-to-all | bytes 442368 | tf_op jit(solution)/shard_map/all_to_all | solution.py:242
  201.8 14.3 %all_to_all.33 = bf16[32,54,128]{2,1,0:T(8,128)(2,1)S(1)} all-to-all(bf16[32,54,128]{2,1,0:T(8,128)(2,1)S(1)} %broadcast_in_dim.75), channel_id=1, replica_groups=mesh['dp'=8,'seq'=32] {'seq'}, dimensions={0} | all-to-all | bytes 884736 | tf_op jit(solution)/shard_map/all_to_all | solution.py:245
  216.3 1.9 slice_reduce_fusion.1
  (169 shorter events, 48.2 us)
Async XLA Ops:
  7.2 47.6 %copy-start = (bf16[768,256]{1,0:T(8,128)(2,1)S(1)}, bf16[768,256]{1,0:T(8,128)(2,1)}, u32[]{:S(2)}) copy-start(bf16[768,256]{1,0:T(8,128)(2,1)} %param.17) | copy-start | bytes 1179652
  8.0 21.5 %collective-permute-start.1 = (s32[16]{0:T(128)S(1)}, s32[16]{0:T(128)S(1)}, u32[]{:S(2)}, u32[]{:S(2)}) collective-permute-start(s32[16]{0:T(128)S(1)} %get-tuple-element.83), channel_id=1, source_target_pairs={{1,0},{2,1},{3,2},{4,3},{5,4},{6,5},{7,6},{8,7},{9,8},{10,9},{11,1... | collective-permute-start | bytes 200 | tf_op jit(solution)/shard_map/ppermute | solution.py:23
  13.1 16.4 %collective-permute-start = (s32[16]{0:T(128)S(1)}, s32[16]{0:T(128)S(1)}, u32[]{:S(2)}, u32[]{:S(2)}) collective-permute-start(s32[16]{0:T(128)S(1)} %get-tuple-element.82), channel_id=1, source_target_pairs={{0,1},{1,2},{2,3},{3,4},{4,5},{5,6},{6,7},{7,8},{8,9},{9,10},{10,1... | collective-permute-start | bytes 200 | tf_op jit(solution)/shard_map/ppermute | solution.py:21
  19.5 24.2 %all-to-all-start = ((s32[32,1,16]{2,1,0:T(1,128)}), s32[32,1,16]{2,1,0:T(1,128)S(1)}, u32[]{:S(2)}, u32[]{:S(2)}) async-start(s32[32,1,16]{2,1,0:T(1,128)} %bitcast.13), calls=%async_computation | async-start | bytes 32768 | tf_op jit(solution)/shard_map/all_to_all | solution.py:119
  36.2 11.4 %copy-start.5 = (bf16[512,768]{1,0:T(8,128)(2,1)}, bf16[512,768]{1,0:T(8,128)(2,1)S(1)}, u32[]{:S(2)}) copy-start(bf16[512,768]{1,0:T(8,128)(2,1)S(1)} %get-tuple-element.87) | copy-start | bytes 2359300
  38.1 7.2 %collective-permute-start.3 = (bf16[128,768]{1,0:T(8,128)(2,1)}, bf16[128,768]{1,0:T(8,128)(2,1)S(1)}, u32[]{:S(2)}, u32[]{:S(2)}) collective-permute-start(bf16[128,768]{1,0:T(8,128)(2,1)} %get-tuple-element.77), channel_id=1, source_target_pairs={{1,0},{2,1},{3,2},{4,3},{5,4},{6,5},{7,6},{8,7},{9,8},{10,9},{11,1... | collective-permute-start | bytes 589832 | tf_op jit(solution)/shard_map/ppermute | solution.py:23
  40.2 6.0 %collective-permute-start.2 = (bf16[128,768]{1,0:T(8,128)(2,1)S(1)}, bf16[128,768]{1,0:T(8,128)(2,1)S(1)}, u32[]{:S(2)}, u32[]{:S(2)}) collective-permute-start(bf16[128,768]{1,0:T(8,128)(2,1)S(1)} %get-tuple-element.76), channel_id=1, source_target_pairs={{0,1},{1,2},{2,3},{3,4},{4,5},{5,6},{6,7},{7,8},{8,9},{9,10},{10,1... | collective-permute-start | bytes 589832 | tf_op jit(solution)/shard_map/ppermute | solution.py:21
  45.1 9.7 %copy-start.24 = (pred[512]{0:T(512)(128)(4,1)}, pred[512]{0:T(512)(128)(4,1)S(1)}, u32[]{:S(2)}) copy-start(pred[512]{0:T(512)(128)(4,1)S(1)} %broadcast_compare_fusion) | copy-start | bytes 1540
  47.6 2.6 %copy-start.6 = (bf16[512,768]{1,0:T(8,128)(2,1)S(1)}, bf16[512,768]{1,0:T(8,128)(2,1)}, u32[]{:S(2)}) copy-start(bf16[512,768]{1,0:T(8,128)(2,1)} %copy-done.5) | copy-start | bytes 2359300
  47.6 3.3 %copy-start.28 = (bf16[2,768,768]{2,1,0:T(8,128)(2,1)S(1)}, bf16[2,768,768]{2,1,0:T(8,128)(2,1)}, u32[]{:S(2)}) copy-start(bf16[2,768,768]{2,1,0:T(8,128)(2,1)} %param.14) | copy-start | bytes 7077892
  52.0 15.3 %copy-start.1 = (bf16[512,768]{1,0:T(8,128)(2,1)}, bf16[512,768]{1,0:T(8,128)(2,1)S(1)}, u32[]{:S(2)}) copy-start(bf16[512,768]{1,0:T(8,128)(2,1)S(1)} %fusion.23) | copy-start | bytes 2359300
  57.0 19.2 %all-to-all-start.1 = ((bf16[32,16,256]{2,1,0:T(8,128)(2,1)}), bf16[32,16,256]{2,1,0:T(8,128)(2,1)}, u32[]{:S(2)}, u32[]{:S(2)}) async-start(bf16[32,16,256]{2,1,0:T(8,128)(2,1)} %bitcast.15), calls=%async_computation.1 | async-start | bytes 524288 | tf_op jit(solution)/shard_map/all_to_all | solution.py:127
  68.5 9.0 %copy-start.22 = (f32[4,256]{1,0:T(4,128)S(1)}, f32[4,256]{1,0:T(4,128)}, u32[]{:S(2)}) copy-start(f32[4,256]{1,0:T(4,128)} %param.18) | copy-start | bytes 12292
  68.5 9.0 %copy-start.23 = (s32[1,256]{1,0:T(1,128)S(1)}, s32[1,256]{1,0:T(1,128)}, u32[]{:S(2)}) copy-start(s32[1,256]{1,0:T(1,128)} %param.22) | copy-start | bytes 3076
  68.5 9.4 %copy-start.26 = (f32[1,256]{1,0:T(1,128)S(1)}, f32[1,256]{1,0:T(1,128)}, u32[]{:S(2)}) copy-start(f32[1,256]{1,0:T(1,128)} %param.23) | copy-start | bytes 3076
  69.8 9.2 %copy-start.19 = (bf16[768,256]{1,0:T(8,128)(2,1)S(1)}, bf16[768,256]{1,0:T(8,128)(2,1)}, u32[]{:S(2)}) copy-start(bf16[768,256]{1,0:T(8,128)(2,1)} %param.16) | copy-start | bytes 1179652
  80.2 12.7 %all-to-all-start.2 = ((bf16[32,16,256]{2,1,0:T(8,128)(2,1)}), bf16[32,16,256]{2,1,0:T(8,128)(2,1)S(1)}, u32[]{:S(2)}, u32[]{:S(2)}) async-start(bf16[32,16,256]{2,1,0:T(8,128)(2,1)} %bitcast.102), calls=%async_computation.2 | async-start | bytes 524288 | tf_op jit(solution)/shard_map/all_to_all | solution.py:151
  84.0 96.3 %reduce-scatter.4.cloned.1.call-start = ((), (), s32[]{:S(2)}) async-start(), calls=%async_computation.6 | async-start | bytes 1990656 | tf_op jit(solution)/shard_map/reduce_scatter | solution.py:238
  87.6 5.7 %copy-start.25 = (pred[512]{0:T(512)(128)(4,1)S(1)}, pred[512]{0:T(512)(128)(4,1)}, u32[]{:S(2)}) copy-start(pred[512]{0:T(512)(128)(4,1)} %copy-done.24) | copy-start | bytes 1540
  94.3 1.9 copy-start.17
  94.3 2.1 copy-start.29
  99.0 7.3 %collective-permute-start.5 = (bf16[128,768]{1,0:T(8,128)(2,1)}, bf16[128,768]{1,0:T(8,128)(2,1)}, u32[]{:S(2)}, u32[]{:S(2)}) collective-permute-start(bf16[128,768]{1,0:T(8,128)(2,1)} %get-tuple-element.75), channel_id=1, source_target_pairs={{1,0},{2,1},{3,2},{4,3},{5,4},{6,5},{7,6},{8,7},{9,8},{10,9},{11,1... | collective-permute-start | bytes 589832 | tf_op jit(solution)/shard_map/ppermute | solution.py:23
  101.1 6.4 %collective-permute-start.4 = (bf16[128,768]{1,0:T(8,128)(2,1)}, bf16[128,768]{1,0:T(8,128)(2,1)}, u32[]{:S(2)}, u32[]{:S(2)}) collective-permute-start(bf16[128,768]{1,0:T(8,128)(2,1)} %get-tuple-element.74), channel_id=1, source_target_pairs={{0,1},{1,2},{2,3},{3,4},{4,5},{5,6},{6,7},{7,8},{8,9},{9,10},{10,1... | collective-permute-start | bytes 589832 | tf_op jit(solution)/shard_map/ppermute | solution.py:21
  105.6 3.3 %copy-start.3 = (f32[768,768]{1,0:T(8,128)S(1)}, f32[768,768]{1,0:T(8,128)}, u32[]{:S(2)}) copy-start(f32[768,768]{1,0:T(8,128)} %copy-done.2) | copy-start | bytes 7077892
  105.6 3.3 %copy-start.7 = (bf16[512,768]{1,0:T(8,128)(2,1)S(1)}, bf16[512,768]{1,0:T(8,128)(2,1)}, u32[]{:S(2)}) copy-start(bf16[512,768]{1,0:T(8,128)(2,1)} %copy-done.5) | copy-start | bytes 2359300
  110.4 2.1 copy-start.30
  114.1 7.7 %copy-start.18 = (f32[512,768]{1,0:T(8,128)S(1)}, f32[512,768]{1,0:T(8,128)}, u32[]{:S(2)}) copy-start(f32[512,768]{1,0:T(8,128)} %copy-done.16) | copy-start | bytes 4718596
  115.1 8.5 %collective-permute-start.7 = (bf16[16,768]{1,0:T(8,128)(2,1)S(1)}, bf16[16,768]{1,0:T(8,128)(2,1)S(1)}, u32[]{:S(2)}, u32[]{:S(2)}) collective-permute-start(bf16[16,768]{1,0:T(8,128)(2,1)S(1)} %get-tuple-element.73), channel_id=1, source_target_pairs={{1,0},{2,1},{3,2},{4,3},{5,4},{6,5},{7,6},{8,7},{9,8},{10,9},{11,1... | collective-permute-start | bytes 73736 | tf_op jit(solution)/shard_map/ppermute | solution.py:23
  117.0 6.0 %copy-start.20 = (bf16[512,768]{1,0:T(8,128)(2,1)S(1)}, bf16[512,768]{1,0:T(8,128)(2,1)}, u32[]{:S(2)}) copy-start(bf16[512,768]{1,0:T(8,128)(2,1)} %gather_fusion.1) | copy-start | bytes 2359300
  117.0 6.5 %collective-permute-start.6 = (bf16[16,768]{1,0:T(8,128)(2,1)S(1)}, bf16[16,768]{1,0:T(8,128)(2,1)S(1)}, u32[]{:S(2)}, u32[]{:S(2)}) collective-permute-start(bf16[16,768]{1,0:T(8,128)(2,1)S(1)} %get-tuple-element.72), channel_id=1, source_target_pairs={{0,1},{1,2},{2,3},{3,4},{4,5},{5,6},{6,7},{7,8},{8,9},{9,10},{10,1... | collective-permute-start | bytes 73736 | tf_op jit(solution)/shard_map/ppermute | solution.py:21
  123.5 2.7 %copy-start.4 = (f32[544,768]{1,0:T(8,128)S(1)}, f32[544,768]{1,0:T(8,128)}, u32[]{:S(2)}) copy-start(f32[544,768]{1,0:T(8,128)} %convert_multiply_fusion.2) | copy-start | bytes 5013508
  131.5 3.9 %collective-permute-start.8 = (bf16[768,1152]{0,1:T(8,128)(2,1)S(1)}, bf16[768,1152]{0,1:T(8,128)(2,1)}, u32[]{:S(2)}, u32[]{:S(2)}) collective-permute-start(bf16[768,1152]{0,1:T(8,128)(2,1)S(1)} %constant_dynamic-slice_fusion), channel_id=1, source_target_pairs={{0,1},{1,0},{2,3},{3,2},{4,5},{5,4},{6,7},{7,6},{8,9},{9,8},{10,11... | collective-permute-start | bytes 5308424 | tf_op jit(solution)/shard_map/ppermute | solution.py:236
  (12 other events, 16.2 us)
Sparse Core Ops, SparseCore 0:
  140.3 39.9 reduce-scatter.3
